TPU v7x, 128 devices: a whole 4x4x4 slice. The times are simulated.
128 devices in a mesh: mp: 8 (over z_hi, y), layer: 4 (over x), example: 4 (over z_lo, core).
Axes of the slice: x: 4, y: 4, z: 4 (z_hi: 2, z_lo: 2; z = z_hi * 2 + z_lo), core: 2. Of those that a mesh axis runs over, the one named last changes fastest.
Arguments:
- cotangent: bfloat16 [4, 2048, 8192], P(None, ('mp', 'layer', 'example')), may hold values from -6 to 6
- down_weight: bfloat16 [4, 14336, 8192], P('layer', 'mp', 'example'), may hold values from -0.0625 to 0.0625
- gate_act: bfloat16 [4, 2048, 14336], P('layer', None, 'mp'), may hold values from -0.25 to 2.5
- layer_input: bfloat16 [4, 2048, 8192], P('layer', ('mp', 'example')), may hold values from -6 to 6
- proj_out: bfloat16 [4, 64, 14336], P('layer', None, 'mp'), may hold values from -0.046875 to 0.046875
- proj_in: bfloat16 [4, 64, 8192], P('layer'), may hold values from -0.0625 to 0.0625
- queries: bfloat16 [4, 1024, 4096], P('layer', ('mp', 'example')), may hold values from -0.09375 to 0.09375
- hessian_prior: float32 [4, 4096, 4096], P('layer', ('mp', 'example')), may hold values from -4 to 4
- doc_lengths: int32 [32], P(('mp', 'example')), may hold values from 16 to 64, as said below
Outputs:
- hessian: float32 [4, 4096, 4096], P('layer', ('mp', 'example'))
- scores: float32 [1024, 32], P(('mp', 'example'))
Inputs may be any that keep to these rules, and one draw needn't show every extreme that they name: Document n holds doc_lengths[n] real tokens at the start of its 64 positions; the rest is padding.
All inputs are finite; a program needn't handle non-finite values.
Results may differ from a plain program's by a relative error of at most 0.0003.
Values may be sent and summed in bfloat16 or wider, within the bound.
No kernel may reach another device: no remote copies, remote signals or barrier semaphores. Data moves between devices by JAX's collectives and lax.ppermute only.
A program may use at most 128 MiB of HBM per device.

v0:
```python
import jax
import jax.numpy as jnp
from jax import lax
from jax.sharding import PartitionSpec as P


def per_device(
    cotangent,
    down_weight,
    gate_act,
    layer_input,
    proj_out,
    proj_in,
    queries,
    hessian_prior,
    doc_lengths,
):
    layer_count, local_rows, model_width = cotangent.shape
    groups = lax.axis_size("example")
    shares = lax.axis_size("mp")
    col_width = model_width // groups
    stacked = lax.all_gather(cotangent, "mp", axis=1, tiled=True)
    pieces = stacked.reshape(layer_count, shares * local_rows, groups, col_width)
    pieces = jnp.transpose(pieces, (0, 2, 1, 3)).reshape(
        layer_count * groups, shares * local_rows, col_width
    )
    routed = lax.all_to_all(pieces, ("layer", "example"), split_axis=0, concat_axis=1, tiled=True)
    ordered = routed.reshape(layer_count * groups, shares, local_rows, col_width)
    token_cols = jnp.swapaxes(ordered, 0, 1).reshape(-1, col_width)
    weight = down_weight[0]
    gate_rows = gate_act[0]
    out_project = proj_out[0].astype(jnp.float32)
    out_width = out_project.shape[0]
    own_rows = layer_input.shape[1]
    hidden_part = lax.dot_general(
        token_cols, weight, (((1,), (1,)), ((), ())), preferred_element_type=jnp.float32
    )
    scaled = hidden_part * gate_rows.astype(jnp.float32)
    out_part = lax.dot_general(
        scaled, out_project, (((1,), (1,)), ((), ())), precision=lax.Precision.HIGHEST
    )
    out_rows = lax.psum_scatter(
        out_part.reshape(lax.axis_size(("mp", "example")) * (own_rows // 2), 2 * out_width),
        ("mp", "example"),
        scatter_dimension=0,
        tiled=True,
    ).reshape(own_rows, out_width)
    in_rows = lax.dot_general(
        layer_input[0], proj_in[0], (((1,), (1,)), ((), ())), preferred_element_type=jnp.float32
    )
    in_width = in_rows.shape[1]
    docs_here = doc_lengths.shape[0]
    seq_len = own_rows // docs_here
    doc_scale = 1.0 / seq_len**0.5
    positions = jnp.arange(seq_len)
    valid_mask = (positions[None, :] < doc_lengths[:, None]).astype(jnp.float32)
    out_docs = out_rows.reshape(docs_here, seq_len, out_width) * valid_mask[:, :, None]
    in_docs = in_rows.reshape(docs_here, seq_len, in_width)
    projected = (
        jnp.einsum("nta,ntb->nab", out_docs, in_docs, precision=lax.Precision.HIGHEST).reshape(
            docs_here, out_width * in_width
        )
        * doc_scale
    )
    all_docs = lax.all_gather(projected, ("mp", "example"), axis=0, tiled=True)
    doc_total = all_docs.shape[0]
    block_rows = hessian_prior.shape[1]
    first_col = lax.axis_index(("mp", "example")) * block_rows
    col_block = lax.dynamic_slice_in_dim(all_docs, first_col, block_rows, 1)
    gram_rows = lax.dot_general(
        col_block, all_docs, (((0,), (0,)), ((), ())), precision=lax.Precision.HIGHEST
    )
    hessian = hessian_prior[0] + gram_rows / doc_total
    score_part = lax.dot_general(
        queries[0].astype(jnp.float32),
        all_docs,
        (((1,), (1,)), ((), ())),
        precision=lax.Precision.HIGHEST,
    )
    scores = lax.psum(score_part, "layer")
    return (hessian[None], scores)


def solution(mesh):
    in_specs = (
        P(None, ("mp", "layer", "example"), None),
        P("layer", "mp", "example"),
        P("layer", None, "mp"),
        P("layer", ("mp", "example"), None),
        P("layer", None, "mp"),
        P("layer", None, None),
        P("layer", ("mp", "example"), None),
        P("layer", ("mp", "example"), None),
        P(("mp", "example")),
    )
    out_specs = (P("layer", ("mp", "example"), None), P(("mp", "example"), None))
    return jax.shard_map(
        per_device, mesh=mesh, in_specs=in_specs, out_specs=out_specs, check_vma=False
    )
```

profile of v0, /device:TPU:0, one launch (start us, length us, event | category | flops | bytes accessed | tf_op | source)
XLA Modules:
  0.0 463.2 jit_solution(17030512316295490414)
XLA Ops:
  7.2 0.0 copy-start
  7.2 0.0 all-gather.3.cloned.1.call-start
  7.2 0.7 all-gather.3.cloned.1.call-update
  7.9 0.0 reduce-scatter.2.cloned.1.call-start
  8.0 113.3 %all-gather.3.cloned.1.call-done = bf16[4,128,8192]{2,1,0:T(8,128)(2,1)} async-done(((bf16[4,16,8192]{2,1,0:T(8,128)(2,1)}), bf16[4,128,8192]{2,1,0:T(8,128)(2,1)}) %all-gather.3.cloned.1.call-update) | async-done | bytes 8388624 | tf_op jit(solution)/shard_map/all_gather | solution.py:22
  121.3 4.0 fusion.15
  125.3 1.0 pad_maximum_fusion
  126.4 99.4 %all_to_all.4 = bf16[16,128,2048]{2,1,0:T(8,128)(2,1)} all-to-all(bf16[16,128,2048]{2,1,0:T(8,128)(2,1)S(1)} %bitcast.46), channel_id=1, replica_groups=mesh['mp'=8,'layer'=4,'example'=4] {'layer','example'}, dimensions={0} | all-to-all | bytes 16777216 | tf_op jit(solution)/shard_map/all_to_all | solution.py:27
  225.8 8.3 %copy.17 = bf16[8,16,16,2048]{3,2,1,0:T(8,128)(2,1)} copy(bf16[8,16,16,2048]{3,2,0,1:T(8,128)(2,1)} %bitcast.47) | data formatting | bytes 16777216 | tf_op jit(solution)/shard_map/transpose | solution.py:29
  234.1 0.0 copy-start.3
  234.1 20.0 %fusion.2 = f32[2048,1792]{1,0:T(8,128)S(1)} fusion(bf16[2048,2048]{1,0:T(8,128)(2,1)} %bitcast.48, bf16[1,1792,2048]{2,1,0:T(8,128)(2,1)} %param.10), kind=kOutput, calls=%fused_computation.4 | convolution fusion | flops 15032385536 | bytes 30408704 | tf_op jit(solution)/shard_map/dot_general | solution.py:35
  254.1 0.0 copy-done.3
  254.1 0.0 copy-start.1
  254.1 0.0 copy-start.2
  254.1 9.6 %fusion = f32[2048,64]{1,0:T(8,128)S(1)} fusion(f32[2048,1792]{1,0:T(8,128)S(1)} %fusion.2, bf16[1,2048,1792]{2,1,0:T(8,128)(2,1)} %param.11, bf16[1,64,1792]{2,1,0:T(8,128)(2,1)S(1)} %copy-done.3), kind=kOutput, calls=%fused_computation.1 | convolution fusion | flops 2825912320 | bytes 22773760 | tf_op jit(solution)/shard_map/dot_general | solution.py:39
  263.7 1.0 reshape.73
  264.7 0.0 reduce-scatter.2.cloned.1.call-update
  265.4 0.1 mul.43
  265.5 0.1 mul.44
  265.6 0.0 copy-done
  265.6 0.0 copy-done.1
  265.6 0.4 fusion.6
  266.0 129.5 %reduce-scatter.2.cloned.1.call-done = f32[32,128]{1,0:T(8,128)} async-done(((f32[1024,128]{1,0:T(8,128)}), f32[32,128]{1,0:T(8,128)}) %reduce-scatter.2.cloned.1.call-update) | async-done | bytes 16400 | tf_op jit(solution)/shard_map/reduce_scatter | solution.py:42
  395.5 0.7 mul.45
  396.3 0.1 mul.46
  396.3 0.2 convolution_multiply_fusion.1
  396.6 0.1 reshape.75
  396.7 36.7 %all-gather = f32[32,1,4096]{2,1,0:T(1,128)S(1)} all-gather(f32[1,1,4096]{2,1,0:T(1,128)S(1)} %reshape.75), channel_id=1, replica_groups=mesh['mp'=8,'layer'=4,'example'=4] {'mp','example'}, dimensions={0}, use_global_device_ids=true | all-gather | bytes 540672 | tf_op jit(solution)/shard_map/all_gather | solution.py:65
  433.3 0.0 copy-done.2
  433.4 0.7 convolution_bitcast_fusion
  434.0 16.9 %psum.7 = f32[32,32]{0,1:T(8,128)S(1)} all-reduce(f32[32,32]{0,1:T(8,128)S(1)} %convolution_bitcast_fusion), channel_id=1, replica_groups=mesh['mp'=8,'layer'=4,'example'=4] {'layer'}, use_global_device_ids=true, to_apply=%region_1.0 | all-reduce | flops 1024 | bytes 8192 | tf_op jit(solution)/shard_map/psum | solution.py:80
  450.9 0.7 copy.19
  451.6 4.8 %fusion.5 = f32[1,128,4096]{2,1,0:T(8,128)} fusion(f32[32,128]{1,0:T(8,128)S(1)} %bitcast.49, f32[1,128,4096]{2,1,0:T(8,128)} %param.16, f32[32,1,4096]{2,1,0:T(1,128)S(1)} %all-gather), kind=kOutput, calls=%fused_computation.8 | convolution fusion | flops 202375168 | bytes 4734976 | tf_op jit(solution)/shard_map/dot_general | solution.py:70
  (2 shorter events, 0.0 us)
Async XLA Ops:
  7.2 258.4 %copy-start = (bf16[1,64,8192]{2,1,0:T(8,128)(2,1)S(1)}, bf16[1,64,8192]{2,1,0:T(8,128)(2,1)}, u32[]{:S(2)}) copy-start(bf16[1,64,8192]{2,1,0:T(8,128)(2,1)} %param.14) | copy-start | bytes 3145732
  7.2 114.1 %all-gather.3.cloned.1.call-start = ((), (), s32[]{:S(2)}) async-start(), calls=%async_computation.2 | async-start | bytes 9437184 | tf_op jit(solution)/shard_map/all_gather | solution.py:22
  7.9 387.6 %reduce-scatter.2.cloned.1.call-start = ((), (), s32[]{:S(2)}) async-start(), calls=%async_computation.3 | async-start | bytes 540672 | tf_op jit(solution)/shard_map/reduce_scatter | solution.py:42
  234.1 20.0 %copy-start.3 = (bf16[1,64,1792]{2,1,0:T(8,128)(2,1)S(1)}, bf16[1,64,1792]{2,1,0:T(8,128)(2,1)}, u32[]{:S(2)}) copy-start(bf16[1,64,1792]{2,1,0:T(8,128)(2,1)} %param.13) | copy-start | bytes 688132
  254.1 11.4 %copy-start.1 = (bf16[1,64,8192]{2,1,0:T(8,128)(2,1)S(1)}, bf16[1,64,8192]{2,1,0:T(8,128)(2,1)}, u32[]{:S(2)}) copy-start(bf16[1,64,8192]{2,1,0:T(8,128)(2,1)} %param.12) | copy-start | bytes 3145732
  254.1 179.2 %copy-start.2 = (bf16[1,32,4096]{2,1,0:T(8,128)(2,1)S(1)}, bf16[1,32,4096]{2,1,0:T(8,128)(2,1)}, u32[]{:S(2)}) copy-start(bf16[1,32,4096]{2,1,0:T(8,128)(2,1)} %param.15) | copy-start | bytes 786436
Sparse Core Ops, SparseCore 0:
  10.3 110.9 all-gather.2
  264.9 130.6 reduce-scatter.1
where the time goes:
time: 464 us; the launch traced here: 463 us
  waiting for transfers between devices  244 us (53%)
  blocking collectives  153 us (33%)
  matrix products  35.7 us (8%)
  between operations  14.8 us (3%)
  local copies, waits for them, and re-layouts  14.3 us (3%)
    reduce_scatter x1, waiting for transfers between devices, per_device(): lax.psum_scatter(out_part.reshape(lax.axis_size(('mp', 'example')) * (own...  130 us
    all_gather x1, waiting for transfers between devices, per_device(): stacked = lax.all_gather(cotangent, 'mp', axis=1, tiled=True)  113 us
    all_to_all x1, blocking collectives, per_device(): lax.all_to_all(pieces, ('layer', 'example'), split_axis=0, concat_axis=1,...  99.4 us
    all_gather x1, blocking collectives, per_device(): all_docs = lax.all_gather(projected, ('mp', 'example'), axis=0, tiled=True)  36.7 us
    dot_general x1, matrix products, per_device(): lax.dot_general(token_cols, weight, (((1,), (1,)), ((), ())), preferred_e...  20 us
    psum x1, blocking collectives, per_device(): scores = lax.psum(score_part, 'layer')  16.9 us
    dot_general x1, matrix products, per_device(): lax.dot_general(scaled, out_project, (((1,), (1,)), ((), ())), precision=...  9.57 us
  transfers between devices with their start and end apart: 2, of which 2 were waited for; matrix products, arithmetic and copies ran while one was open for 0% of the time, Pallas kernels for 0%

commit v1 on v0

--- a/solution.py
+++ b/solution.py
@@ -19,14 +19,15 @@
     groups = lax.axis_size("example")
     shares = lax.axis_size("mp")
     col_width = model_width // groups
-    stacked = lax.all_gather(cotangent, "mp", axis=1, tiled=True)
-    pieces = stacked.reshape(layer_count, shares * local_rows, groups, col_width)
-    pieces = jnp.transpose(pieces, (0, 2, 1, 3)).reshape(
-        layer_count * groups, shares * local_rows, col_width
+    pieces = cotangent.reshape(layer_count, local_rows, groups, col_width)
+    pieces = jnp.transpose(pieces, (0, 2, 1, 3))
+    pieces = jnp.broadcast_to(pieces[None], (shares,) + pieces.shape).reshape(
+        shares * layer_count * groups, local_rows, col_width
     )
-    routed = lax.all_to_all(pieces, ("layer", "example"), split_axis=0, concat_axis=1, tiled=True)
-    ordered = routed.reshape(layer_count * groups, shares, local_rows, col_width)
-    token_cols = jnp.swapaxes(ordered, 0, 1).reshape(-1, col_width)
+    routed = lax.all_to_all(
+        pieces, ("mp", "layer", "example"), split_axis=0, concat_axis=1, tiled=True
+    )
+    token_cols = routed.reshape(-1, col_width)
     weight = down_weight[0]
     gate_rows = gate_act[0]
     out_project = proj_out[0].astype(jnp.float32)
@@ -39,12 +40,15 @@
     out_part = lax.dot_general(
         scaled, out_project, (((1,), (1,)), ((), ())), precision=lax.Precision.HIGHEST
     )
-    out_rows = lax.psum_scatter(
-        out_part.reshape(lax.axis_size(("mp", "example")) * (own_rows // 2), 2 * out_width),
+    doc_devices = lax.axis_size(("mp", "example"))
+    gathered = lax.all_to_all(
+        out_part.reshape(doc_devices, own_rows, out_width),
         ("mp", "example"),
-        scatter_dimension=0,
+        split_axis=0,
+        concat_axis=0,
         tiled=True,
-    ).reshape(own_rows, out_width)
+    )
+    out_rows = jnp.sum(gathered, axis=0)
     in_rows = lax.dot_general(
         layer_input[0], proj_in[0], (((1,), (1,)), ((), ())), preferred_element_type=jnp.float32
     )
@@ -77,7 +81,7 @@
         (((1,), (1,)), ((), ())),
         precision=lax.Precision.HIGHEST,
     )
-    scores = lax.psum(score_part, "layer")
+    scores = jnp.sum(lax.all_gather(score_part, "layer", axis=0), axis=0)
     return (hessian[None], scores)
 
 

time: 464 us -> 231 us (0.50)
  waiting for transfers between devices: 244 us -> 11 us
  between operations: 14.8 us -> 1.43 us
  starting transfers between devices: 0.08 us -> 12.2 us
  local copies, waits for them, and re-layouts: 14.3 us -> 6.15 us
  blocking collectives: 153 us -> 159 us
    reduce_scatter x1 -> x0, waiting for transfers between devices: 130 us -> none  [per_device(): lax.psum_scatter(out_part.reshape(lax.axis_size(('mp', 'example')) * (own...]
    all_gather x1 -> x0, waiting for transfers between devices: 113 us -> none  [per_device(): stacked = lax.all_gather(cotangent, 'mp', axis=1, tiled=True)]
    psum x1 -> x0, blocking collectives: 16.9 us -> none  [per_device(): scores = lax.psum(score_part, 'layer')]
    all_gather x0 -> x1, blocking collectives: none -> 13.1 us  [per_device(): scores = jnp.sum(lax.all_gather(score_part, 'layer', axis=0), axis=0)]
    all_to_all x0 -> x1, starting transfers between devices: none -> 12.2 us  [per_device(): lax.all_to_all(out_part.reshape(doc_devices, own_rows, out_width), ('mp',...]
    all_to_all x0 -> x1, waiting for transfers between devices: none -> 11 us  [per_device(): lax.all_to_all(out_part.reshape(doc_devices, own_rows, out_width), ('mp',...]
    all_to_all x1, blocking collectives: 99.4 us -> 108 us  [per_device(): lax.all_to_all(pieces, ('mp', 'layer', 'example'), split_axis=0, concat_a...]
    transpose x1, local copies, waits for them, and re-layouts: 8.26 us -> 0.58 us  [per_device(): pieces = jnp.transpose(pieces, (0, 2, 1, 3))]
  transfers between devices with their start and end apart: 2 -> 1, of which waited for: 2 -> 1; matrix products, arithmetic and copies ran while one was open for 0% -> 0% of each run, Pallas kernels for 0% -> 0%
where the time goes in v1:
time: 231 us; the launch traced here: 230 us
  blocking collectives  159 us (69%)
  matrix products  38.2 us (17%)
  starting transfers between devices  12.2 us (5%)
  waiting for transfers between devices  11 us (5%)
  local copies, waits for them, and re-layouts  6.15 us (3%)
  other arithmetic  2.6 us (1%)
    all_to_all x1, blocking collectives, per_device(): lax.all_to_all(pieces, ('mp', 'layer', 'example'), split_axis=0, concat_a...  108 us
    all_gather x1, blocking collectives, per_device(): all_docs = lax.all_gather(projected, ('mp', 'example'), axis=0, tiled=True)  37.6 us
    dot_general x1, matrix products, per_device(): lax.dot_general(token_cols, weight, (((1,), (1,)), ((), ())), preferred_e...  21.6 us
    all_gather x1, blocking collectives, per_device(): scores = jnp.sum(lax.all_gather(score_part, 'layer', axis=0), axis=0)  13.1 us
    all_to_all x1, starting transfers between devices, per_device(): lax.all_to_all(out_part.reshape(doc_devices, own_rows, out_width), ('mp',...  12.2 us
    all_to_all x1, waiting for transfers between devices, per_device(): lax.all_to_all(out_part.reshape(doc_devices, own_rows, out_width), ('mp',...  11 us
    dot_general x1, matrix products, per_device(): lax.dot_general(scaled, out_project, (((1,), (1,)), ((), ())), precision=...  10.3 us
    dot_general x1, matrix products, per_device(): lax.dot_general(col_block, all_docs, (((0,), (0,)), ((), ())), precision=...  4.82 us
  transfers between devices with their start and end apart: 1, of which 1 were waited for; matrix products, arithmetic and copies ran while one was open for 0% of the time, Pallas kernels for 0%

profile of v1, /device:TPU:0, one launch (start us, length us, event | category | flops | bytes accessed | tf_op | source)
XLA Modules:
  0.0 230.4 jit_solution(13786707926677547751)
XLA Ops:
  0.6 0.0 copy-start
  0.6 1.9 reshape.74
  2.6 0.6 copy.16
  3.2 1.1 broadcast_in_dim.4
  4.2 108.1 %all_to_all.14 = bf16[128,16,2048]{2,1,0:T(8,128)(2,1)S(1)} all-to-all(bf16[128,16,2048]{2,1,0:T(8,128)(2,1)S(1)} %bitcast.42), channel_id=1, replica_groups=mesh['mp'=8,'layer'=4,'example'=4] {'mp','layer','example'}, dimensions={0} | all-to-all | bytes 16777216 | tf_op jit(solution)/shard_map/all_to_all | solution.py:27
  112.4 0.0 copy-start.3
  112.4 21.6 %convert_multiply_fusion = f32[2048,1792]{1,0:T(8,128)} fusion(bf16[2048,2048]{1,0:T(8,128)(2,1)S(1)} %bitcast.44, bf16[1,2048,1792]{2,1,0:T(8,128)(2,1)} %param.11, bf16[1,1792,2048]{2,1,0:T(8,128)(2,1)} %param.10), kind=kOutput, calls=%fused_computation | convolution fusion | flops 15039725568 | bytes 37748736 | tf_op jit(solution)/shard_map/dot_general | solution.py:36
  134.0 0.0 copy-done.3
  134.0 0.0 copy-start.1
  134.0 10.3 %fusion.11 = f32[32,64,64]{2,1,0:T(8,128)S(1)} fusion(f32[32,64,1792]{2,1,0:T(8,128)} %bitcast.43, bf16[1,64,1792]{2,1,0:T(8,128)(2,1)S(1)} %copy-done.3), kind=kOutput, calls=%fused_computation.15 | convolution fusion | flops 2818572288 | bytes 15433728 | tf_op jit(solution)/shard_map/dot_general | solution.py:40
  144.4 0.0 copy-start.2
  144.4 1.4 reshape.84
  145.8 12.2 %all-to-all-start.1 = ((f32[32,1,4096]{2,1,0:T(1,128)}), f32[32,1,4096]{2,1,0:T(1,128)S(1)}, u32[]{:S(2)}, u32[]{:S(2)}) async-start(f32[32,1,4096]{2,1,0:T(1,128)} %reshape.84), calls=%async_computation.1 | async-start | bytes 1048576 | tf_op jit(solution)/shard_map/all_to_all | solution.py:44
  158.7 0.0 copy-done
  158.7 0.0 copy-done.1
  158.7 0.4 fusion.3
  159.2 11.0 %all-to-all-done.1 = f32[32,1,4096]{2,1,0:T(1,128)S(1)} async-done(((f32[32,1,4096]{2,1,0:T(1,128)}), f32[32,1,4096]{2,1,0:T(1,128)S(1)}, u32[]{:S(2)}, u32[]{:S(2)}) %all-to-all-start.1) | async-done | bytes 524320 | tf_op jit(solution)/shard_map/all_to_all | solution.py:44
  170.1 0.5 broadcast.29
  170.6 1.9 reduce
  172.5 0.4 reshape.85
  173.0 0.1 reduce_sum.18
  173.0 0.3 convolution_multiply_fusion.1
  173.4 0.1 reshape.79
  173.4 37.6 %all-gather.1 = f32[32,1,4096]{2,1,0:T(1,128)S(1)} all-gather(f32[1,1,4096]{2,1,0:T(1,128)S(1)} %reshape.79), channel_id=1, replica_groups=mesh['mp'=8,'layer'=4,'example'=4] {'mp','example'}, dimensions={0}, use_global_device_ids=true | all-gather | bytes 540672 | tf_op jit(solution)/shard_map/all_gather | solution.py:69
  211.1 0.0 copy-done.2
  211.1 0.7 convolution_bitcast_fusion
  211.8 0.1 copy.17
  211.9 13.1 %all-gather = f32[128,32]{1,0:T(8,128)S(1)} all-gather(f32[32,32]{1,0:T(8,128)S(1)} %copy.17), channel_id=2, replica_groups=mesh['mp'=8,'layer'=4,'example'=4] {'layer'}, dimensions={0}, use_global_device_ids=true | all-gather | bytes 20480 | tf_op jit(solution)/shard_map/all_gather | solution.py:84
  225.0 0.6 reduce_sum.19
  225.6 4.8 %fusion.2 = f32[1,128,4096]{2,1,0:T(8,128)} fusion(f32[32,128]{1,0:T(8,128)S(1)} %bitcast.47, f32[1,128,4096]{2,1,0:T(8,128)} %param.16, f32[32,1,4096]{2,1,0:T(1,128)S(1)} %all-gather.1), kind=kOutput, calls=%fused_computation.4 | convolution fusion | flops 202375168 | bytes 4734976 | tf_op jit(solution)/shard_map/dot_general | solution.py:74
  (2 shorter events, 0.0 us)
Async XLA Ops:
  0.6 158.1 %copy-start = (bf16[1,64,8192]{2,1,0:T(8,128)(2,1)S(1)}, bf16[1,64,8192]{2,1,0:T(8,128)(2,1)}, u32[]{:S(2)}) copy-start(bf16[1,64,8192]{2,1,0:T(8,128)(2,1)} %param.14) | copy-start | bytes 3145732
  112.4 21.6 %copy-start.3 = (bf16[1,64,1792]{2,1,0:T(8,128)(2,1)S(1)}, bf16[1,64,1792]{2,1,0:T(8,128)(2,1)}, u32[]{:S(2)}) copy-start(bf16[1,64,1792]{2,1,0:T(8,128)(2,1)} %param.13) | copy-start | bytes 688132
  134.0 24.7 %copy-start.1 = (bf16[1,64,8192]{2,1,0:T(8,128)(2,1)S(1)}, bf16[1,64,8192]{2,1,0:T(8,128)(2,1)}, u32[]{:S(2)}) copy-start(bf16[1,64,8192]{2,1,0:T(8,128)(2,1)} %param.12) | copy-start | bytes 3145732
  144.4 66.7 %copy-start.2 = (bf16[1,32,4096]{2,1,0:T(8,128)(2,1)S(1)}, bf16[1,32,4096]{2,1,0:T(8,128)(2,1)}, u32[]{:S(2)}) copy-start(bf16[1,32,4096]{2,1,0:T(8,128)(2,1)} %param.15) | copy-start | bytes 786436
  145.8 24.3 %all-to-all-start.1 = ((f32[32,1,4096]{2,1,0:T(1,128)}), f32[32,1,4096]{2,1,0:T(1,128)S(1)}, u32[]{:S(2)}, u32[]{:S(2)}) async-start(f32[32,1,4096]{2,1,0:T(1,128)} %reshape.84), calls=%async_computation.1 | async-start | bytes 1048576 | tf_op jit(solution)/shard_map/all_to_all | solution.py:44

commit v2 on v1

--- a/solution.py
+++ b/solution.py
@@ -2,6 +2,42 @@
 import jax.numpy as jnp
 from jax import lax
 from jax.sharding import PartitionSpec as P
+from jax.experimental import pallas as pl
+from jax.experimental.pallas import tpu as pltpu
+
+
+def _up_kernel(cot_ref, w_ref, gate_ref, proj_ref, out_ref):
+    hidden = lax.dot_general(
+        cot_ref[...], w_ref[...], (((1,), (1,)), ((), ())), preferred_element_type=jnp.float32
+    )
+    scaled = hidden * gate_ref[...].astype(jnp.float32)
+    high = scaled.astype(jnp.bfloat16)
+    low = (scaled - high.astype(jnp.float32)).astype(jnp.bfloat16)
+    proj = proj_ref[...]
+    dims = (((1,), (1,)), ((), ()))
+    out_ref[...] = lax.dot_general(
+        high, proj, dims, preferred_element_type=jnp.float32
+    ) + lax.dot_general(low, proj, dims, preferred_element_type=jnp.float32)
+
+
+def _up_project(token_cols, weight, gate_rows, proj):
+    tokens, feats = token_cols.shape
+    hidden = weight.shape[0]
+    width = proj.shape[0]
+    tile = 256
+    return pl.pallas_call(
+        _up_kernel,
+        grid=(tokens // tile,),
+        in_specs=[
+            pl.BlockSpec((tile, feats), lambda i: (i, 0)),
+            pl.BlockSpec((hidden, feats), lambda i: (0, 0)),
+            pl.BlockSpec((tile, hidden), lambda i: (i, 0)),
+            pl.BlockSpec((width, hidden), lambda i: (0, 0)),
+        ],
+        out_specs=pl.BlockSpec((tile, width), lambda i: (i, 0)),
+        out_shape=jax.ShapeDtypeStruct((tokens, width), jnp.float32),
+        compiler_params=pltpu.CompilerParams(vmem_limit_bytes=48 * 1024 * 1024),
+    )(token_cols, weight, gate_rows, proj)
 
 
 def per_device(
@@ -28,18 +64,9 @@
         pieces, ("mp", "layer", "example"), split_axis=0, concat_axis=1, tiled=True
     )
     token_cols = routed.reshape(-1, col_width)
-    weight = down_weight[0]
-    gate_rows = gate_act[0]
-    out_project = proj_out[0].astype(jnp.float32)
-    out_width = out_project.shape[0]
+    out_width = proj_out.shape[1]
     own_rows = layer_input.shape[1]
-    hidden_part = lax.dot_general(
-        token_cols, weight, (((1,), (1,)), ((), ())), preferred_element_type=jnp.float32
-    )
-    scaled = hidden_part * gate_rows.astype(jnp.float32)
-    out_part = lax.dot_general(
-        scaled, out_project, (((1,), (1,)), ((), ())), precision=lax.Precision.HIGHEST
-    )
+    out_part = _up_project(token_cols, down_weight[0], gate_act[0], proj_out[0])
     doc_devices = lax.axis_size(("mp", "example"))
     gathered = lax.all_to_all(
         out_part.reshape(doc_devices, own_rows, out_width),
@@ -66,7 +93,13 @@
         )
         * doc_scale
     )
-    all_docs = lax.all_gather(projected, ("mp", "example"), axis=0, tiled=True)
+    all_docs = lax.all_to_all(
+        jnp.broadcast_to(projected, (doc_devices, projected.shape[1])),
+        ("mp", "example"),
+        split_axis=0,
+        concat_axis=0,
+        tiled=True,
+    )
     doc_total = all_docs.shape[0]
     block_rows = hessian_prior.shape[1]
     first_col = lax.axis_index(("mp", "example")) * block_rows
@@ -81,7 +114,17 @@
         (((1,), (1,)), ((), ())),
         precision=lax.Precision.HIGHEST,
     )
-    scores = jnp.sum(lax.all_gather(score_part, "layer", axis=0), axis=0)
+    layers = lax.axis_size("layer")
+    scores = jnp.sum(
+        lax.all_to_all(
+            jnp.broadcast_to(score_part[None], (layers,) + score_part.shape),
+            "layer",
+            split_axis=0,
+            concat_axis=0,
+            tiled=True,
+        ),
+        axis=0,
+    )
     return (hessian[None], scores)
 
 

time: 231 us -> 202 us (0.87)
  blocking collectives: 159 us -> 108 us
  matrix products: 38.2 us -> 6.21 us
  Pallas kernels: 0 us -> 29.3 us
  waiting for transfers between devices: 11 us -> 23.9 us
  starting transfers between devices: 12.2 us -> 21.3 us
    all_gather x2 -> x0, blocking collectives: 50.7 us -> none  [the longest x1 37.6 us: per_device(): all_docs = lax.all_gather(projected, ('mp', 'example'), axis=0, tiled=True)]
    dot_general x2 -> x0, matrix products: 32 us -> none  [the longest x1 21.6 us: per_device(): lax.dot_general(token_cols, weight, (((1,), (1,)), ((), ())), preferred_e...]
    pallas_call x0 -> x1, Pallas kernels: none -> 29.3 us  [_up_project(): pl.pallas_call(_up_kernel, grid=(tokens // tile,), in_specs=[pl.BlockSpec...]
    all_to_all x0 -> x2, waiting for transfers between devices: none -> 12.8 us  [the longest x1 12.2 us: per_device(): lax.all_to_all(jnp.broadcast_to(projected, (doc_devices, projected.shape[...]
    all_to_all x0 -> x2, starting transfers between devices: none -> 9.19 us  [the longest x1 5.3 us: per_device(): lax.all_to_all(jnp.broadcast_to(score_part[None], (layers,) + score_part....]
  transfers between devices with their start and end apart: 1 -> 3, of which waited for: 1 -> 3; matrix products, arithmetic and copies ran while one was open for 0% -> 3% of each run, Pallas kernels for 0% -> 0%
where the time goes in v2:
time: 202 us
  blocking collectives  108 us (53%)
  Pallas kernels  29.3 us (15%)
  waiting for transfers between devices  23.9 us (12%)
  starting transfers between devices  21.3 us (11%)
  local copies, waits for them, and re-layouts  8.27 us (4%)
  matrix products  6.21 us (3%)
  other arithmetic  3.38 us (2%)
    all_to_all x1, blocking collectives, per_device(): lax.all_to_all(pieces, ('mp', 'layer', 'example'), split_axis=0, concat_a...  108 us
    pallas_call x1, Pallas kernels, _up_project(): pl.pallas_call(_up_kernel, grid=(tokens // tile,), in_specs=[pl.BlockSpec...  29.3 us
    all_to_all x1, waiting for transfers between devices, per_device(): lax.all_to_all(jnp.broadcast_to(projected, (doc_devices, projected.shape[...  12.2 us
    all_to_all x1, starting transfers between devices, per_device(): lax.all_to_all(out_part.reshape(doc_devices, own_rows, out_width), ('mp',...  12.1 us
    all_to_all x1, waiting for transfers between devices, per_device(): lax.all_to_all(out_part.reshape(doc_devices, own_rows, out_width), ('mp',...  11.1 us
    all_to_all x1, starting transfers between devices, per_device(): lax.all_to_all(jnp.broadcast_to(score_part[None], (layers,) + score_part....  5.3 us
    dot_general x1, matrix products, per_device(): lax.dot_general(col_block, all_docs, (((0,), (0,)), ((), ())), precision=...  4.83 us
  transfers between devices with their start and end apart: 3, of which 3 were waited for; matrix products, arithmetic and copies ran while one was open for 3% of the time, Pallas kernels for 0%

profile of v2, /device:TPU:0, one launch (start us, length us, event | category | flops | bytes accessed | tf_op | source)
XLA Modules:
  0.0 202.0 jit_solution(514166750164371003)
XLA Ops:
  0.6 0.0 copy-start
  0.6 1.9 reshape.76
  2.6 0.6 copy.13
  3.2 1.1 broadcast_in_dim.8
  4.2 0.0 copy-start.1
  4.2 108.3 %all_to_all.28 = bf16[128,16,2048]{2,1,0:T(8,128)(2,1)} all-to-all(bf16[128,16,2048]{2,1,0:T(8,128)(2,1)S(1)} %bitcast.34), channel_id=1, replica_groups=mesh['mp'=8,'layer'=4,'example'=4] {'mp','layer','example'}, dimensions={0} | all-to-all | bytes 16777216 | tf_op jit(solution)/shard_map/all_to_all | solution.py:63
  112.5 0.0 copy-done.1
  112.5 29.3 %shard_map.104 = f32[2048,64]{1,0:T(8,128)S(1)} custom-call(bf16[2048,2048]{1,0:T(8,128)(2,1)} %bitcast.35, bf16[1792,2048]{1,0:T(8,128)(2,1)} %bitcast.36, bf16[2048,1792]{1,0:T(8,128)(2,1)} %bitcast.37, bf16[64,1792]{1,0:T(8,128)(2,1)S(1)} %bitcast.33), custom_call_target="tpu_custom_call" | custom-call | tf_op jit(solution)/shard_map/pallas_call | solution.py:28
  141.8 0.0 copy-start.2
  141.8 1.4 reshape.80
  143.2 12.1 %all-to-all-start.1 = ((f32[32,1,4096]{2,1,0:T(1,128)}), f32[32,1,4096]{2,1,0:T(1,128)S(1)}, u32[]{:S(2)}, u32[]{:S(2)}) async-start(f32[32,1,4096]{2,1,0:T(1,128)} %reshape.80), calls=%async_computation.1 | async-start | bytes 1048576 | tf_op jit(solution)/shard_map/all_to_all | solution.py:71
  156.0 0.0 copy-done
  156.0 0.0 copy-done.2
  156.0 0.4 fusion.2
  156.4 11.1 %all-to-all-done.1 = f32[32,1,4096]{2,1,0:T(1,128)S(1)} async-done(((f32[32,1,4096]{2,1,0:T(1,128)}), f32[32,1,4096]{2,1,0:T(1,128)S(1)}, u32[]{:S(2)}, u32[]{:S(2)}) %all-to-all-start.1) | async-done | bytes 524320 | tf_op jit(solution)/shard_map/all_to_all | solution.py:71
  167.6 0.6 broadcast.31
  168.2 1.9 reduce
  170.1 0.0 copy-start.3
  170.1 0.4 reshape.81
  170.5 0.1 reduce_sum.18
  170.6 0.3 convolution_multiply_fusion.1
  170.9 0.1 mul.39
  171.0 1.3 broadcast_in_dim.9
  172.3 3.9 %all-to-all-start.2 = ((f32[32,1,4096]{2,1,0:T(1,128)}), f32[32,1,4096]{2,1,0:T(1,128)S(1)}, u32[]{:S(2)}, u32[]{:S(2)}) async-start(f32[32,1,4096]{2,1,0:T(1,128)} %broadcast_in_dim.9), calls=%async_computation.2 | async-start | bytes 1048576 | tf_op jit(solution)/shard_map/all_to_all | solution.py:96
  176.2 12.2 %all-to-all-done.2 = f32[32,1,4096]{2,1,0:T(1,128)S(1)} async-done(((f32[32,1,4096]{2,1,0:T(1,128)}), f32[32,1,4096]{2,1,0:T(1,128)S(1)}, u32[]{:S(2)}, u32[]{:S(2)}) %all-to-all-start.2) | async-done | bytes 524320 | tf_op jit(solution)/shard_map/all_to_all | solution.py:96
  188.4 0.0 copy-done.3
  188.4 0.7 convolution_bitcast_fusion
  189.1 0.1 copy.14
  189.2 0.7 reshape.82
  189.9 5.3 %all-to-all-start.3 = ((f32[4,1,1024]{2,1,0:T(1,128)}), f32[4,1,1024]{2,1,0:T(1,128)S(1)}, u32[]{:S(2)}, u32[]{:S(2)}) async-start(f32[4,1,1024]{2,1,0:T(1,128)} %reshape.82), calls=%async_computation.3 | async-start | bytes 32768 | tf_op jit(solution)/shard_map/all_to_all | solution.py:119
  195.2 4.8 %fusion.1 = f32[1,128,4096]{2,1,0:T(8,128)} fusion(f32[32,128]{1,0:T(8,128)S(1)} %bitcast.39, f32[1,128,4096]{2,1,0:T(8,128)} %param.16, f32[32,1,4096]{2,1,0:T(1,128)S(1)} %all-to-all-done.2), kind=kOutput, calls=%fused_computation.2 | convolution fusion | flops 202375168 | bytes 4734976 | tf_op jit(solution)/shard_map/dot_general | solution.py:107
  200.0 0.5 all-to-all-done.3
  200.6 0.7 reduce.1
  201.3 0.1 reshape.83
  201.4 0.6 reduce_sum.19
  (3 shorter events, 0.0 us)
Async XLA Ops:
  0.6 155.4 %copy-start = (bf16[1,64,8192]{2,1,0:T(8,128)(2,1)S(1)}, bf16[1,64,8192]{2,1,0:T(8,128)(2,1)}, u32[]{:S(2)}) copy-start(bf16[1,64,8192]{2,1,0:T(8,128)(2,1)} %param.14) | copy-start | bytes 3145732
  4.2 108.3 %copy-start.1 = (bf16[1,64,1792]{2,1,0:T(8,128)(2,1)S(1)}, bf16[1,64,1792]{2,1,0:T(8,128)(2,1)}, u32[]{:S(2)}) copy-start(bf16[1,64,1792]{2,1,0:T(8,128)(2,1)} %param.13) | copy-start | bytes 688132
  141.8 14.2 %copy-start.2 = (bf16[1,64,8192]{2,1,0:T(8,128)(2,1)S(1)}, bf16[1,64,8192]{2,1,0:T(8,128)(2,1)}, u32[]{:S(2)}) copy-start(bf16[1,64,8192]{2,1,0:T(8,128)(2,1)} %param.12) | copy-start | bytes 3145732
  143.2 24.3 %all-to-all-start.1 = ((f32[32,1,4096]{2,1,0:T(1,128)}), f32[32,1,4096]{2,1,0:T(1,128)S(1)}, u32[]{:S(2)}, u32[]{:S(2)}) async-start(f32[32,1,4096]{2,1,0:T(1,128)} %reshape.80), calls=%async_computation.1 | async-start | bytes 1048576 | tf_op jit(solution)/shard_map/all_to_all | solution.py:71
  170.1 18.3 %copy-start.3 = (bf16[1,32,4096]{2,1,0:T(8,128)(2,1)S(1)}, bf16[1,32,4096]{2,1,0:T(8,128)(2,1)}, u32[]{:S(2)}) copy-start(bf16[1,32,4096]{2,1,0:T(8,128)(2,1)} %param.15) | copy-start | bytes 786436
  172.3 16.2 %all-to-all-start.2 = ((f32[32,1,4096]{2,1,0:T(1,128)}), f32[32,1,4096]{2,1,0:T(1,128)S(1)}, u32[]{:S(2)}, u32[]{:S(2)}) async-start(f32[32,1,4096]{2,1,0:T(1,128)} %broadcast_in_dim.9), calls=%async_computation.2 | async-start | bytes 1048576 | tf_op jit(solution)/shard_map/all_to_all | solution.py:96
  189.9 10.7 %all-to-all-start.3 = ((f32[4,1,1024]{2,1,0:T(1,128)}), f32[4,1,1024]{2,1,0:T(1,128)S(1)}, u32[]{:S(2)}, u32[]{:S(2)}) async-start(f32[4,1,1024]{2,1,0:T(1,128)} %reshape.82), calls=%async_computation.3 | async-start | bytes 32768 | tf_op jit(solution)/shard_map/all_to_all | solution.py:119

commit v3 on v2

--- a/solution.py
+++ b/solution.py
@@ -10,7 +10,8 @@
     hidden = lax.dot_general(
         cot_ref[...], w_ref[...], (((1,), (1,)), ((), ())), preferred_element_type=jnp.float32
     )
-    scaled = hidden * gate_ref[...].astype(jnp.float32)
+    gate = gate_ref[...].astype(jnp.float32).reshape(hidden.shape)
+    scaled = hidden * gate
     high = scaled.astype(jnp.bfloat16)
     low = (scaled - high.astype(jnp.float32)).astype(jnp.bfloat16)
     proj = proj_ref[...]
@@ -20,24 +21,26 @@
     ) + lax.dot_general(low, proj, dims, preferred_element_type=jnp.float32)
 
 
-def _up_project(token_cols, weight, gate_rows, proj):
+def _up_project(token_cols, weight, gate4, chunk, proj):
     tokens, feats = token_cols.shape
     hidden = weight.shape[0]
     width = proj.shape[0]
+    chunk_rows = gate4.shape[2]
     tile = 256
+    per_tile = tile // chunk_rows
     return pl.pallas_call(
         _up_kernel,
         grid=(tokens // tile,),
         in_specs=[
             pl.BlockSpec((tile, feats), lambda i: (i, 0)),
             pl.BlockSpec((hidden, feats), lambda i: (0, 0)),
-            pl.BlockSpec((tile, hidden), lambda i: (i, 0)),
+            pl.BlockSpec((per_tile, None, chunk_rows, hidden), lambda i: (i, chunk, 0, 0)),
             pl.BlockSpec((width, hidden), lambda i: (0, 0)),
         ],
         out_specs=pl.BlockSpec((tile, width), lambda i: (i, 0)),
         out_shape=jax.ShapeDtypeStruct((tokens, width), jnp.float32),
         compiler_params=pltpu.CompilerParams(vmem_limit_bytes=48 * 1024 * 1024),
-    )(token_cols, weight, gate_rows, proj)
+    )(token_cols, weight, gate4, proj)
 
 
 def per_device(
@@ -55,18 +58,27 @@
     groups = lax.axis_size("example")
     shares = lax.axis_size("mp")
     col_width = model_width // groups
-    pieces = cotangent.reshape(layer_count, local_rows, groups, col_width)
-    pieces = jnp.transpose(pieces, (0, 2, 1, 3))
-    pieces = jnp.broadcast_to(pieces[None], (shares,) + pieces.shape).reshape(
-        shares * layer_count * groups, local_rows, col_width
-    )
-    routed = lax.all_to_all(
-        pieces, ("mp", "layer", "example"), split_axis=0, concat_axis=1, tiled=True
-    )
-    token_cols = routed.reshape(-1, col_width)
+    chunks = 2
+    chunk_rows = local_rows // chunks
+    pieces = cotangent.reshape(layer_count, chunks, chunk_rows, groups, col_width)
+    pieces = jnp.transpose(pieces, (1, 0, 3, 2, 4))
+    sources = shares * layer_count * groups
     out_width = proj_out.shape[1]
     own_rows = layer_input.shape[1]
-    out_part = _up_project(token_cols, down_weight[0], gate_act[0], proj_out[0])
+    gate4 = gate_act[0].reshape(sources, chunks, chunk_rows, gate_act.shape[2])
+    outs = []
+    for c in range(chunks):
+        piece = jnp.broadcast_to(pieces[c][None], (shares,) + pieces.shape[1:]).reshape(
+            sources, chunk_rows, col_width
+        )
+        routed = lax.all_to_all(
+            piece, ("mp", "layer", "example"), split_axis=0, concat_axis=0, tiled=True
+        )
+        outs.append(
+            _up_project(routed.reshape(-1, col_width), down_weight[0], gate4, c, proj_out[0])
+        )
+    out_part = jnp.stack(outs).reshape(chunks, sources, chunk_rows, out_width)
+    out_part = jnp.transpose(out_part, (1, 0, 2, 3)).reshape(-1, out_width)
     doc_devices = lax.axis_size(("mp", "example"))
     gathered = lax.all_to_all(
         out_part.reshape(doc_devices, own_rows, out_width),

time: 202 us -> 200 us (0.990)
  blocking collectives: 108 us -> 63.7 us
  waiting for transfers between devices: 23.9 us -> 56.5 us
  Pallas kernels: 29.3 us -> 32.7 us
  local copies, waits for them, and re-layouts: 8.27 us -> 11.2 us
  starting transfers between devices: 21.3 us -> 23.4 us
    all_to_all x1, blocking collectives: 108 us -> 63.7 us  [per_device(): lax.all_to_all(piece, ('mp', 'layer', 'example'), split_axis=0, concat_ax...]
    all_to_all x0 -> x1, waiting for transfers between devices: none -> 33.8 us  [per_device(): lax.all_to_all(piece, ('mp', 'layer', 'example'), split_axis=0, concat_ax...]
    all_to_all x0 -> x1, starting transfers between devices: none -> 9.26 us  [per_device(): lax.all_to_all(piece, ('mp', 'layer', 'example'), split_axis=0, concat_ax...]
    all_to_all x1, starting transfers between devices: 12.1 us -> 5.09 us  [per_device(): lax.all_to_all(out_part.reshape(doc_devices, own_rows, out_width), ('mp',...]
    pallas_call x1 -> x2, Pallas kernels: 29.3 us -> 32.7 us  [_up_project(): pl.pallas_call(_up_kernel, grid=(tokens // tile,), in_specs=[pl.BlockSpec...]
    broadcast_in_dim x1 -> x3, local copies, waits for them, and re-layouts: 1.05 us -> 4.4 us  [per_device(): jnp.broadcast_to(pieces[c][None], (shares,) + pieces.shape[1:])]
    unnamed x12, local copies, waits for them, and re-layouts: 2.68 us -> 4.85 us
  transfers between devices with their start and end apart: 3 -> 4, of which waited for: 3 -> 4; matrix products, arithmetic and copies ran while one was open for 3% -> 3% of each run, Pallas kernels for 0% -> 8%
where the time goes in v3:
time: 200 us
  blocking collectives  63.7 us (32%)
  waiting for transfers between devices  56.5 us (28%)
  Pallas kernels  32.7 us (16%)
  starting transfers between devices  23.4 us (12%)
  local copies, waits for them, and re-layouts  11.2 us (6%)
  matrix products  7.43 us (4%)
  other arithmetic  3.34 us (2%)
    all_to_all x1, blocking collectives, per_device(): lax.all_to_all(piece, ('mp', 'layer', 'example'), split_axis=0, concat_ax...  63.7 us
    all_to_all x1, waiting for transfers between devices, per_device(): lax.all_to_all(piece, ('mp', 'layer', 'example'), split_axis=0, concat_ax...  33.8 us
    pallas_call x2, Pallas kernels, _up_project(): pl.pallas_call(_up_kernel, grid=(tokens // tile,), in_specs=[pl.BlockSpec...  32.7 us
    all_to_all x1, waiting for transfers between devices, per_device(): lax.all_to_all(jnp.broadcast_to(projected, (doc_devices, projected.shape[...  12.2 us
    all_to_all x1, waiting for transfers between devices, per_device(): lax.all_to_all(out_part.reshape(doc_devices, own_rows, out_width), ('mp',...  9.93 us
    all_to_all x1, starting transfers between devices, per_device(): lax.all_to_all(piece, ('mp', 'layer', 'example'), split_axis=0, concat_ax...  9.26 us
    all_to_all x1, starting transfers between devices, per_device(): lax.all_to_all(jnp.broadcast_to(score_part[None], (layers,) + score_part....  5.2 us
    all_to_all x1, starting transfers between devices, per_device(): lax.all_to_all(out_part.reshape(doc_devices, own_rows, out_width), ('mp',...  5.09 us
  transfers between devices with their start and end apart: 4, of which 4 were waited for; matrix products, arithmetic and copies ran while one was open for 3% of the time, Pallas kernels for 8%

profile of v3, /device:TPU:0, one launch (start us, length us, event | category | flops | bytes accessed | tf_op | source)
XLA Modules:
  0.0 199.7 jit_solution(3061301680397488901)
XLA Ops:
  0.6 0.0 copy-start
  0.6 1.4 slice_bitcast_fusion.1
  2.0 0.5 broadcast_in_dim.15
  2.6 63.7 %all_to_all.29 = bf16[128,8,2048]{2,1,0:T(8,128)(2,1)} all-to-all(bf16[128,8,2048]{2,1,0:T(8,128)(2,1)S(1)} %bitcast.58), channel_id=1, replica_groups=mesh['mp'=8,'layer'=4,'example'=4] {'mp','layer','example'}, dimensions={0} | all-to-all | bytes 8388608 | tf_op jit(solution)/shard_map/all_to_all | solution.py:74
  66.2 2.5 %broadcast_in_dim.34 = bf16[8,4,4,8,2048]{4,3,2,1,0:T(8,128)(2,1)} broadcast(bf16[4,4,8,2048]{3,2,1,0:T(8,128)(2,1)S(1)} %get-tuple-element.3), dimensions={1,2,3,4} | broadcast | bytes 4718592 | tf_op jit(solution)/shard_map/broadcast_in_dim | solution.py:71
  68.7 0.0 copy-start.2
  68.7 9.3 %all-to-all-start.1 = ((bf16[128,8,2048]{2,1,0:T(8,128)(2,1)}), bf16[128,8,2048]{2,1,0:T(8,128)(2,1)}, u32[]{:S(2)}, u32[]{:S(2)}) async-start(bf16[128,8,2048]{2,1,0:T(8,128)(2,1)} %bitcast.57), calls=%async_computation.1 | async-start | bytes 8388608 | tf_op jit(solution)/shard_map/all_to_all | solution.py:74
  78.0 0.0 copy-done.2
  78.0 0.0 copy-start.1
  78.0 2.2 %copy-done.1 = bf16[128,8,2048]{2,1,0:T(8,128)(2,1)S(1)} copy-done((bf16[128,8,2048]{2,1,0:T(8,128)(2,1)S(1)}, bf16[128,8,2048]{2,1,0:T(8,128)(2,1)}, u32[]{:S(2)}) %copy-start.1) | copy-done | bytes 4194328
  80.2 16.1 %shard_map.104 = f32[1024,64]{1,0:T(8,128)S(1)} custom-call(bf16[1024,2048]{1,0:T(8,128)(2,1)S(1)} %bitcast.48, bf16[1792,2048]{1,0:T(8,128)(2,1)} %bitcast.53, bf16[128,2,8,1792]{3,2,1,0:T(8,128)(2,1)} %bitcast.55, bf16[64,1792]{1,0:T(8,128)(2,1)S(1)} %bitcast.51), custom_call_target="tpu_custom_call" | custom-call | tf_op jit(solution)/shard_map/pallas_call | solution.py:31
  96.3 33.8 %all-to-all-done.1 = bf16[128,8,2048]{2,1,0:T(8,128)(2,1)} async-done(((bf16[128,8,2048]{2,1,0:T(8,128)(2,1)}), bf16[128,8,2048]{2,1,0:T(8,128)(2,1)}, u32[]{:S(2)}, u32[]{:S(2)}) %all-to-all-start.1) | async-done | bytes 4194336 | tf_op jit(solution)/shard_map/all_to_all | solution.py:74
  130.1 16.5 %shard_map.105 = f32[1024,64]{1,0:T(8,128)S(1)} custom-call(bf16[1024,2048]{1,0:T(8,128)(2,1)} %bitcast.14.cot_ref, bf16[1792,2048]{1,0:T(8,128)(2,1)} %bitcast.54, bf16[128,2,8,1792]{3,2,1,0:T(8,128)(2,1)} %bitcast.56, bf16[64,1792]{1,0:T(8,128)(2,1)S(1)} %bitcast.52), custom_call_target="tpu_custom_call" | custom-call | tf_op jit(solution)/shard_map/pallas_call | solution.py:31
  146.7 0.1 pad_maximum_fusion
  146.8 1.4 reshape.84
  148.2 5.1 %all-to-all-start.2 = ((f32[32,1,4096]{2,1,0:T(1,128)}), f32[32,1,4096]{2,1,0:T(1,128)S(1)}, u32[]{:S(2)}, u32[]{:S(2)}) async-start(f32[32,1,4096]{2,1,0:T(1,128)} %reshape.84), calls=%async_computation.2 | async-start | bytes 1048576 | tf_op jit(solution)/shard_map/all_to_all | solution.py:83
  154.0 0.0 copy-done
  154.0 1.6 fusion.2
  155.6 9.9 %all-to-all-done.2 = f32[32,1,4096]{2,1,0:T(1,128)S(1)} async-done(((f32[32,1,4096]{2,1,0:T(1,128)}), f32[32,1,4096]{2,1,0:T(1,128)S(1)}, u32[]{:S(2)}, u32[]{:S(2)}) %all-to-all-start.2) | async-done | bytes 524320 | tf_op jit(solution)/shard_map/all_to_all | solution.py:83
  165.6 0.5 broadcast.30
  166.1 1.9 reduce
  168.0 0.0 copy-start.3
  168.0 0.4 reshape.85
  168.4 0.1 reduce_sum.18
  168.5 0.3 convolution_multiply_fusion.1
  168.8 0.1 mul.39
  168.9 1.3 broadcast_in_dim.35
  170.2 3.9 %all-to-all-start.3 = ((f32[32,1,4096]{2,1,0:T(1,128)}), f32[32,1,4096]{2,1,0:T(1,128)S(1)}, u32[]{:S(2)}, u32[]{:S(2)}) async-start(f32[32,1,4096]{2,1,0:T(1,128)} %broadcast_in_dim.35), calls=%async_computation.3 | async-start | bytes 1048576 | tf_op jit(solution)/shard_map/all_to_all | solution.py:108
  174.1 12.2 %all-to-all-done.3 = f32[32,1,4096]{2,1,0:T(1,128)S(1)} async-done(((f32[32,1,4096]{2,1,0:T(1,128)}), f32[32,1,4096]{2,1,0:T(1,128)S(1)}, u32[]{:S(2)}, u32[]{:S(2)}) %all-to-all-start.3) | async-done | bytes 524320 | tf_op jit(solution)/shard_map/all_to_all | solution.py:108
  186.3 0.0 copy-done.3
  186.3 0.7 convolution_bitcast_fusion
  187.0 0.1 copy.17
  187.1 0.7 reshape.86
  187.8 5.2 %all-to-all-start.4 = ((f32[4,1,1024]{2,1,0:T(1,128)}), f32[4,1,1024]{2,1,0:T(1,128)S(1)}, u32[]{:S(2)}, u32[]{:S(2)}) async-start(f32[4,1,1024]{2,1,0:T(1,128)} %reshape.86), calls=%async_computation.4 | async-start | bytes 32768 | tf_op jit(solution)/shard_map/all_to_all | solution.py:131
  193.0 4.8 %fusion.1 = f32[1,128,4096]{2,1,0:T(8,128)} fusion(f32[32,128]{1,0:T(8,128)S(1)} %bitcast.61, f32[1,128,4096]{2,1,0:T(8,128)} %param.16, f32[32,1,4096]{2,1,0:T(1,128)S(1)} %all-to-all-done.3), kind=kOutput, calls=%fused_computation.2 | convolution fusion | flops 202375168 | bytes 4734976 | tf_op jit(solution)/shard_map/dot_general | solution.py:119
  197.8 0.5 all-to-all-done.4
  198.3 0.7 reduce.1
  199.0 0.1 reshape.87
  199.1 0.6 reduce_sum.19
  (3 shorter events, 0.0 us)
Async XLA Ops:
  0.6 153.3 %copy-start = (bf16[1,64,8192]{2,1,0:T(8,128)(2,1)S(1)}, bf16[1,64,8192]{2,1,0:T(8,128)(2,1)}, u32[]{:S(2)}) copy-start(bf16[1,64,8192]{2,1,0:T(8,128)(2,1)} %param.14) | copy-start | bytes 3145732
  68.7 9.3 %copy-start.2 = (bf16[1,64,1792]{2,1,0:T(8,128)(2,1)S(1)}, bf16[1,64,1792]{2,1,0:T(8,128)(2,1)}, u32[]{:S(2)}) copy-start(bf16[1,64,1792]{2,1,0:T(8,128)(2,1)} %param.13) | copy-start | bytes 688132
  68.7 61.4 %all-to-all-start.1 = ((bf16[128,8,2048]{2,1,0:T(8,128)(2,1)}), bf16[128,8,2048]{2,1,0:T(8,128)(2,1)}, u32[]{:S(2)}, u32[]{:S(2)}) async-start(bf16[128,8,2048]{2,1,0:T(8,128)(2,1)} %bitcast.57), calls=%async_computation.1 | async-start | bytes 8388608 | tf_op jit(solution)/shard_map/all_to_all | solution.py:74
  78.0 2.2 %copy-start.1 = (bf16[128,8,2048]{2,1,0:T(8,128)(2,1)S(1)}, bf16[128,8,2048]{2,1,0:T(8,128)(2,1)}, u32[]{:S(2)}) copy-start(bf16[128,8,2048]{2,1,0:T(8,128)(2,1)} %all_to_all.29) | copy-start | bytes 12582916
  148.2 17.4 %all-to-all-start.2 = ((f32[32,1,4096]{2,1,0:T(1,128)}), f32[32,1,4096]{2,1,0:T(1,128)S(1)}, u32[]{:S(2)}, u32[]{:S(2)}) async-start(f32[32,1,4096]{2,1,0:T(1,128)} %reshape.84), calls=%async_computation.2 | async-start | bytes 1048576 | tf_op jit(solution)/shard_map/all_to_all | solution.py:83
  168.0 18.3 %copy-start.3 = (bf16[1,32,4096]{2,1,0:T(8,128)(2,1)S(1)}, bf16[1,32,4096]{2,1,0:T(8,128)(2,1)}, u32[]{:S(2)}) copy-start(bf16[1,32,4096]{2,1,0:T(8,128)(2,1)} %param.15) | copy-start | bytes 786436
  170.2 16.2 %all-to-all-start.3 = ((f32[32,1,4096]{2,1,0:T(1,128)}), f32[32,1,4096]{2,1,0:T(1,128)S(1)}, u32[]{:S(2)}, u32[]{:S(2)}) async-start(f32[32,1,4096]{2,1,0:T(1,128)} %broadcast_in_dim.35), calls=%async_computation.3 | async-start | bytes 1048576 | tf_op jit(solution)/shard_map/all_to_all | solution.py:108
  187.8 10.6 %all-to-all-start.4 = ((f32[4,1,1024]{2,1,0:T(1,128)}), f32[4,1,1024]{2,1,0:T(1,128)S(1)}, u32[]{:S(2)}, u32[]{:S(2)}) async-start(f32[4,1,1024]{2,1,0:T(1,128)} %reshape.86), calls=%async_computation.4 | async-start | bytes 32768 | tf_op jit(solution)/shard_map/all_to_all | solution.py:131

commit v4 on v2

--- a/solution.py
+++ b/solution.py
@@ -10,7 +10,11 @@
     hidden = lax.dot_general(
         cot_ref[...], w_ref[...], (((1,), (1,)), ((), ())), preferred_element_type=jnp.float32
     )
-    scaled = hidden * gate_ref[...].astype(jnp.float32)
+    layers, groups = gate_ref.shape[1], gate_ref.shape[2]
+    gate = jnp.concatenate(
+        [gate_ref[0, l, e] for e in range(groups) for l in range(layers)], axis=0
+    ).astype(jnp.float32)
+    scaled = hidden * gate
     high = scaled.astype(jnp.bfloat16)
     low = (scaled - high.astype(jnp.float32)).astype(jnp.bfloat16)
     proj = proj_ref[...]
@@ -20,24 +24,25 @@
     ) + lax.dot_general(low, proj, dims, preferred_element_type=jnp.float32)
 
 
-def _up_project(token_cols, weight, gate_rows, proj):
+def _up_project(token_cols, weight, gate5, proj):
     tokens, feats = token_cols.shape
     hidden = weight.shape[0]
     width = proj.shape[0]
-    tile = 256
+    blocks, layers, groups, rows = gate5.shape[:4]
+    tile = tokens // blocks
     return pl.pallas_call(
         _up_kernel,
-        grid=(tokens // tile,),
+        grid=(blocks,),
         in_specs=[
             pl.BlockSpec((tile, feats), lambda i: (i, 0)),
             pl.BlockSpec((hidden, feats), lambda i: (0, 0)),
-            pl.BlockSpec((tile, hidden), lambda i: (i, 0)),
+            pl.BlockSpec((1, layers, groups, rows, hidden), lambda i: (i, 0, 0, 0, 0)),
             pl.BlockSpec((width, hidden), lambda i: (0, 0)),
         ],
         out_specs=pl.BlockSpec((tile, width), lambda i: (i, 0)),
         out_shape=jax.ShapeDtypeStruct((tokens, width), jnp.float32),
         compiler_params=pltpu.CompilerParams(vmem_limit_bytes=48 * 1024 * 1024),
-    )(token_cols, weight, gate_rows, proj)
+    )(token_cols, weight, gate5, proj)
 
 
 def per_device(
@@ -56,17 +61,21 @@
     shares = lax.axis_size("mp")
     col_width = model_width // groups
     pieces = cotangent.reshape(layer_count, local_rows, groups, col_width)
-    pieces = jnp.transpose(pieces, (0, 2, 1, 3))
+    pieces = jnp.transpose(pieces, (2, 0, 1, 3))
     pieces = jnp.broadcast_to(pieces[None], (shares,) + pieces.shape).reshape(
-        shares * layer_count * groups, local_rows, col_width
+        shares * groups * layer_count, local_rows, col_width
     )
     routed = lax.all_to_all(
-        pieces, ("mp", "layer", "example"), split_axis=0, concat_axis=1, tiled=True
+        pieces, ("mp", "example", "layer"), split_axis=0, concat_axis=0, tiled=True
     )
     token_cols = routed.reshape(-1, col_width)
     out_width = proj_out.shape[1]
     own_rows = layer_input.shape[1]
-    out_part = _up_project(token_cols, down_weight[0], gate_act[0], proj_out[0])
+    gate5 = gate_act[0].reshape(shares, layer_count, groups, local_rows, gate_act.shape[2])
+    out_part = _up_project(token_cols, down_weight[0], gate5, proj_out[0])
+    out_part = jnp.transpose(
+        out_part.reshape(shares, groups, layer_count, local_rows, out_width), (0, 2, 1, 3, 4)
+    ).reshape(-1, out_width)
     doc_devices = lax.axis_size(("mp", "example"))
     gathered = lax.all_to_all(
         out_part.reshape(doc_devices, own_rows, out_width),

time: 202 us -> 193 us (0.955)
  starting transfers between devices: 21.3 us -> 12.1 us
    all_to_all x1, starting transfers between devices: 12.1 us -> 4.18 us  [per_device(): lax.all_to_all(out_part.reshape(doc_devices, own_rows, out_width), ('mp',...]
where the time goes in v4:
time: 193 us
  blocking collectives  108 us (56%)
  Pallas kernels  29.3 us (15%)
  waiting for transfers between devices  23.9 us (12%)
  starting transfers between devices  12.1 us (6%)
  local copies, waits for them, and re-layouts  8.41 us (4%)
  matrix products  6.21 us (3%)
  other arithmetic  3.38 us (2%)
    all_to_all x1, blocking collectives, per_device(): lax.all_to_all(pieces, ('mp', 'example', 'layer'), split_axis=0, concat_a...  108 us
    pallas_call x1, Pallas kernels, _up_project(): pl.pallas_call(_up_kernel, grid=(blocks,), in_specs=[pl.BlockSpec((tile,...  29.3 us
    all_to_all x1, waiting for transfers between devices, per_device(): lax.all_to_all(jnp.broadcast_to(projected, (doc_devices, projected.shape[...  12.2 us
    all_to_all x1, waiting for transfers between devices, per_device(): lax.all_to_all(out_part.reshape(doc_devices, own_rows, out_width), ('mp',...  11.1 us
    dot_general x1, matrix products, per_device(): lax.dot_general(col_block, all_docs, (((0,), (0,)), ((), ())), precision=...  4.83 us
    all_to_all x1, starting transfers between devices, per_device(): lax.all_to_all(out_part.reshape(doc_devices, own_rows, out_width), ('mp',...  4.18 us
    all_to_all x1, starting transfers between devices, per_device(): lax.all_to_all(jnp.broadcast_to(score_part[None], (layers,) + score_part....  4.05 us
    all_to_all x1, starting transfers between devices, per_device(): lax.all_to_all(jnp.broadcast_to(projected, (doc_devices, projected.shape[...  3.89 us
  transfers between devices with their start and end apart: 3, of which 3 were waited for; matrix products, arithmetic and copies ran while one was open for 3% of the time, Pallas kernels for 0%

profile of v4, /device:TPU:0, one launch (start us, length us, event | category | flops | bytes accessed | tf_op | source)
XLA Modules:
  0.0 192.6 jit_solution(16804021024034358210)
XLA Ops:
  0.6 0.0 copy-start
  0.6 1.9 %reshape.72 = bf16[4,16,4,2048]{3,2,1,0:T(4,128)(2,1)S(1)} reshape(bf16[4,16,8192]{2,1,0:T(8,128)(2,1)} %param.9) | data formatting | bytes 2097152 | tf_op jit(solution)/shard_map/reshape | solution.py:63
  2.6 0.6 copy.16
  3.2 1.1 broadcast_in_dim.8
  4.2 0.0 copy-start.1
  4.2 107.9 %all_to_all.24 = bf16[128,16,2048]{2,1,0:T(8,128)(2,1)} all-to-all(bf16[128,16,2048]{2,1,0:T(8,128)(2,1)S(1)} %bitcast.37), channel_id=1, replica_groups=mesh['mp'=8,'layer'=4,'example'=4] {'mp','example','layer'}, dimensions={0} | all-to-all | bytes 16777216 | tf_op jit(solution)/shard_map/all_to_all | solution.py:68
  112.1 0.0 copy-done.1
  112.1 29.3 %shard_map.104 = f32[2048,64]{1,0:T(8,128)S(1)} custom-call(bf16[2048,2048]{1,0:T(8,128)(2,1)} %bitcast.38, bf16[1792,2048]{1,0:T(8,128)(2,1)} %bitcast.39, bf16[8,4,4,16,1792]{4,3,2,1,0:T(8,128)(2,1)} %bitcast.40, bf16[64,1792]{1,0:T(8,128)(2,1)S(1)} %bitcast.36), custom_call_target="tpu_custom_call" | custom-call | tf_op jit(solution)/shard_map/pallas_call | solution.py:33
  141.4 0.0 copy-start.2
  141.4 0.1 copy.17
  141.5 1.5 reshape.76
  143.0 4.2 %all-to-all-start.1 = ((f32[32,1,4096]{2,1,0:T(1,128)}), f32[32,1,4096]{2,1,0:T(1,128)S(1)}, u32[]{:S(2)}, u32[]{:S(2)}) async-start(f32[32,1,4096]{2,1,0:T(1,128)} %reshape.76), calls=%async_computation.1 | async-start | bytes 1048576 | tf_op jit(solution)/shard_map/all_to_all | solution.py:80
  147.8 0.0 copy-done
  147.8 0.0 copy-done.2
  147.9 0.4 fusion.2
  148.3 11.1 %all-to-all-done.1 = f32[32,1,4096]{2,1,0:T(1,128)S(1)} async-done(((f32[32,1,4096]{2,1,0:T(1,128)}), f32[32,1,4096]{2,1,0:T(1,128)S(1)}, u32[]{:S(2)}, u32[]{:S(2)}) %all-to-all-start.1) | async-done | bytes 524320 | tf_op jit(solution)/shard_map/all_to_all | solution.py:80
  159.4 0.6 broadcast.31
  160.0 1.9 %reduce = f32[32,4096]{1,0:T(8,128)S(1)} reduce(f32[32,1,4096]{2,1,0:T(1,128)S(1)} %all-to-all-done.1, f32[]{:T(128)} %broadcast.31), dimensions={1}, to_apply=%all_to_all.16.reduce_sub_computation | reduce | bytes 1048580 | tf_op jit(solution)/shard_map/all_to_all | solution.py:80
  162.0 0.0 copy-start.3
  162.0 0.4 reshape.77
  162.4 0.1 reduce_sum.18
  162.5 0.3 convolution_multiply_fusion.1
  162.8 0.1 mul.39
  162.9 1.3 broadcast_in_dim.9
  164.1 3.9 %all-to-all-start.2 = ((f32[32,1,4096]{2,1,0:T(1,128)}), f32[32,1,4096]{2,1,0:T(1,128)S(1)}, u32[]{:S(2)}, u32[]{:S(2)}) async-start(f32[32,1,4096]{2,1,0:T(1,128)} %broadcast_in_dim.9), calls=%async_computation.2 | async-start | bytes 1048576 | tf_op jit(solution)/shard_map/all_to_all | solution.py:105
  168.0 12.2 %all-to-all-done.2 = f32[32,1,4096]{2,1,0:T(1,128)S(1)} async-done(((f32[32,1,4096]{2,1,0:T(1,128)}), f32[32,1,4096]{2,1,0:T(1,128)S(1)}, u32[]{:S(2)}, u32[]{:S(2)}) %all-to-all-start.2) | async-done | bytes 524320 | tf_op jit(solution)/shard_map/all_to_all | solution.py:105
  180.3 0.0 copy-done.3
  180.3 0.7 convolution_bitcast_fusion
  181.0 0.1 copy.18
  181.0 0.7 reshape.78
  181.8 4.0 %all-to-all-start.3 = ((f32[4,1,1024]{2,1,0:T(1,128)}), f32[4,1,1024]{2,1,0:T(1,128)S(1)}, u32[]{:S(2)}, u32[]{:S(2)}) async-start(f32[4,1,1024]{2,1,0:T(1,128)} %reshape.78), calls=%async_computation.3 | async-start | bytes 32768 | tf_op jit(solution)/shard_map/all_to_all | solution.py:128
  185.8 4.8 %fusion.1 = f32[1,128,4096]{2,1,0:T(8,128)} fusion(f32[32,128]{1,0:T(8,128)S(1)} %bitcast.43, f32[1,128,4096]{2,1,0:T(8,128)} %param.16, f32[32,1,4096]{2,1,0:T(1,128)S(1)} %all-to-all-done.2), kind=kOutput, calls=%fused_computation.2 | convolution fusion | flops 202375168 | bytes 4734976 | tf_op jit(solution)/shard_map/dot_general | solution.py:116
  190.7 0.5 all-to-all-done.3
  191.2 0.7 reduce.1
  191.9 0.1 reshape.79
  192.0 0.6 reduce_sum.19
  (3 shorter events, 0.0 us)
Async XLA Ops:
  0.6 147.2 %copy-start = (bf16[1,64,8192]{2,1,0:T(8,128)(2,1)S(1)}, bf16[1,64,8192]{2,1,0:T(8,128)(2,1)}, u32[]{:S(2)}) copy-start(bf16[1,64,8192]{2,1,0:T(8,128)(2,1)} %param.14) | copy-start | bytes 3145732
  4.2 107.9 %copy-start.1 = (bf16[1,64,1792]{2,1,0:T(8,128)(2,1)S(1)}, bf16[1,64,1792]{2,1,0:T(8,128)(2,1)}, u32[]{:S(2)}) copy-start(bf16[1,64,1792]{2,1,0:T(8,128)(2,1)} %param.13) | copy-start | bytes 688132
  141.4 6.5 %copy-start.2 = (bf16[1,64,8192]{2,1,0:T(8,128)(2,1)S(1)}, bf16[1,64,8192]{2,1,0:T(8,128)(2,1)}, u32[]{:S(2)}) copy-start(bf16[1,64,8192]{2,1,0:T(8,128)(2,1)} %param.12) | copy-start | bytes 3145732
  143.0 16.4 %all-to-all-start.1 = ((f32[32,1,4096]{2,1,0:T(1,128)}), f32[32,1,4096]{2,1,0:T(1,128)S(1)}, u32[]{:S(2)}, u32[]{:S(2)}) async-start(f32[32,1,4096]{2,1,0:T(1,128)} %reshape.76), calls=%async_computation.1 | async-start | bytes 1048576 | tf_op jit(solution)/shard_map/all_to_all | solution.py:80
  162.0 18.3 %copy-start.3 = (bf16[1,32,4096]{2,1,0:T(8,128)(2,1)S(1)}, bf16[1,32,4096]{2,1,0:T(8,128)(2,1)}, u32[]{:S(2)}) copy-start(bf16[1,32,4096]{2,1,0:T(8,128)(2,1)} %param.15) | copy-start | bytes 786436
  164.1 16.1 %all-to-all-start.2 = ((f32[32,1,4096]{2,1,0:T(1,128)}), f32[32,1,4096]{2,1,0:T(1,128)S(1)}, u32[]{:S(2)}, u32[]{:S(2)}) async-start(f32[32,1,4096]{2,1,0:T(1,128)} %broadcast_in_dim.9), calls=%async_computation.2 | async-start | bytes 1048576 | tf_op jit(solution)/shard_map/all_to_all | solution.py:105
  181.8 9.4 %all-to-all-start.3 = ((f32[4,1,1024]{2,1,0:T(1,128)}), f32[4,1,1024]{2,1,0:T(1,128)S(1)}, u32[]{:S(2)}, u32[]{:S(2)}) async-start(f32[4,1,1024]{2,1,0:T(1,128)} %reshape.78), calls=%async_computation.3 | async-start | bytes 32768 | tf_op jit(solution)/shard_map/all_to_all | solution.py:128

commit v5 on v2

--- a/solution.py
+++ b/solution.py
@@ -1,3 +1,5 @@
+import functools
+
 import jax
 import jax.numpy as jnp
 from jax import lax
@@ -6,11 +8,19 @@
 from jax.experimental.pallas import tpu as pltpu
 
 
-def _up_kernel(cot_ref, w_ref, gate_ref, proj_ref, out_ref):
+def _up_kernel(cot_ref, w_ref, gate_ref, proj_ref, out_ref, *, layer_major, lo, hi):
     hidden = lax.dot_general(
         cot_ref[...], w_ref[...], (((1,), (1,)), ((), ())), preferred_element_type=jnp.float32
     )
-    scaled = hidden * gate_ref[...].astype(jnp.float32)
+    blocks, layers, groups = gate_ref.shape[:3]
+    if layer_major:
+        order = [(b, l, e) for b in range(blocks) for l in range(layers) for e in range(groups)]
+    else:
+        order = [(b, l, e) for b in range(blocks) for e in range(groups) for l in range(layers)]
+    gate = jnp.concatenate(
+        [gate_ref[b, l, e].astype(jnp.float32)[lo:hi] for b, l, e in order], axis=0
+    )
+    scaled = hidden * gate
     high = scaled.astype(jnp.bfloat16)
     low = (scaled - high.astype(jnp.float32)).astype(jnp.bfloat16)
     proj = proj_ref[...]
@@ -20,24 +30,27 @@
     ) + lax.dot_general(low, proj, dims, preferred_element_type=jnp.float32)
 
 
-def _up_project(token_cols, weight, gate_rows, proj):
+def _up_project(token_cols, weight, gate5, proj, layer_major, lo, hi):
     tokens, feats = token_cols.shape
     hidden = weight.shape[0]
     width = proj.shape[0]
-    tile = 256
+    shares, layers, groups, rows = gate5.shape[:4]
+    per_tile = 2
+    tile = tokens // shares * per_tile
+    kernel = functools.partial(_up_kernel, layer_major=layer_major, lo=lo, hi=hi)
     return pl.pallas_call(
-        _up_kernel,
-        grid=(tokens // tile,),
+        kernel,
+        grid=(shares // per_tile,),
         in_specs=[
             pl.BlockSpec((tile, feats), lambda i: (i, 0)),
             pl.BlockSpec((hidden, feats), lambda i: (0, 0)),
-            pl.BlockSpec((tile, hidden), lambda i: (i, 0)),
+            pl.BlockSpec((per_tile, layers, groups, rows, hidden), lambda i: (i, 0, 0, 0, 0)),
             pl.BlockSpec((width, hidden), lambda i: (0, 0)),
         ],
         out_specs=pl.BlockSpec((tile, width), lambda i: (i, 0)),
         out_shape=jax.ShapeDtypeStruct((tokens, width), jnp.float32),
         compiler_params=pltpu.CompilerParams(vmem_limit_bytes=48 * 1024 * 1024),
-    )(token_cols, weight, gate_rows, proj)
+    )(token_cols, weight, gate5, proj)
 
 
 def per_device(
@@ -55,18 +68,32 @@
     groups = lax.axis_size("example")
     shares = lax.axis_size("mp")
     col_width = model_width // groups
-    pieces = cotangent.reshape(layer_count, local_rows, groups, col_width)
-    pieces = jnp.transpose(pieces, (0, 2, 1, 3))
-    pieces = jnp.broadcast_to(pieces[None], (shares,) + pieces.shape).reshape(
-        shares * layer_count * groups, local_rows, col_width
-    )
-    routed = lax.all_to_all(
-        pieces, ("mp", "layer", "example"), split_axis=0, concat_axis=1, tiled=True
-    )
-    token_cols = routed.reshape(-1, col_width)
+    split = local_rows // 2
     out_width = proj_out.shape[1]
     own_rows = layer_input.shape[1]
-    out_part = _up_project(token_cols, down_weight[0], gate_act[0], proj_out[0])
+    gate5 = gate_act[0].reshape(shares, layer_count, groups, local_rows, gate_act.shape[2])
+    near = cotangent[:, :split].reshape(layer_count, split, groups, col_width)
+    near = jnp.transpose(near, (0, 2, 1, 3)).reshape(layer_count * groups, split, col_width)
+    near = lax.all_to_all(near, ("layer", "example"), split_axis=0, concat_axis=0, tiled=True)
+    near = lax.all_gather(near, "mp", axis=0, tiled=True)
+    rest = local_rows - split
+    far = cotangent[:, split:].reshape(layer_count, rest, groups, col_width)
+    far = jnp.transpose(far, (2, 0, 1, 3))
+    far = jnp.broadcast_to(far[None], (shares,) + far.shape).reshape(
+        shares * groups * layer_count, rest, col_width
+    )
+    far = lax.all_to_all(far, ("mp", "example", "layer"), split_axis=0, concat_axis=0, tiled=True)
+    far_out = _up_project(
+        far.reshape(-1, col_width), down_weight[0], gate5, proj_out[0], False, split, local_rows
+    )
+    near_out = _up_project(
+        near.reshape(-1, col_width), down_weight[0], gate5, proj_out[0], True, 0, split
+    )
+    far_out = jnp.transpose(
+        far_out.reshape(shares, groups, layer_count, rest, out_width), (0, 2, 1, 3, 4)
+    )
+    near_out = near_out.reshape(shares, layer_count, groups, split, out_width)
+    out_part = jnp.concatenate([near_out, far_out], axis=3).reshape(-1, out_width)
     doc_devices = lax.axis_size(("mp", "example"))
     gathered = lax.all_to_all(
         out_part.reshape(doc_devices, own_rows, out_width),

time: 202 us -> 217 us (1.074)
  waiting for transfers between devices: 23.9 us -> 57.8 us
  blocking collectives: 108 us -> 80.2 us
  between operations: 1.45 us -> 14.9 us
  starting transfers between devices: 21.3 us -> 12.1 us
  Pallas kernels: 29.3 us -> 32.9 us
    all_gather x0 -> x1, waiting for transfers between devices: none -> 33.9 us  [per_device(): near = lax.all_gather(near, 'mp', axis=0, tiled=True)]
    all_to_all x1 -> x2, blocking collectives: 108 us -> 80.2 us  [the longest x1 63.4 us: per_device(): lax.all_to_all(far, ('mp', 'example', 'layer'), split_axis=0, concat_axis...]
    all_to_all x1, starting transfers between devices: 12.1 us -> 3.89 us  [per_device(): lax.all_to_all(out_part.reshape(doc_devices, own_rows, out_width), ('mp',...]
    pallas_call x1 -> x2, Pallas kernels: 29.3 us -> 32.9 us  [_up_project(): pl.pallas_call(kernel, grid=(shares // per_tile,), in_specs=[pl.BlockSpec...]
    unnamed x12 -> x14, local copies, waits for them, and re-layouts: 2.68 us -> 4.87 us
  transfers between devices with their start and end apart: 3 -> 4, of which waited for: 3 -> 4; matrix products, arithmetic and copies ran while one was open for 3% -> 3% of each run, Pallas kernels for 0% -> 8%
where the time goes in v5:
time: 217 us; the launch traced here: 216 us
  blocking collectives  80.2 us (37%)
  waiting for transfers between devices  57.8 us (27%)
  Pallas kernels  32.9 us (15%)
  between operations  14.9 us (7%)
  starting transfers between devices  12.1 us (6%)
  local copies, waits for them, and re-layouts  8.63 us (4%)
  matrix products  6.21 us (3%)
  other arithmetic  3.26 us (2%)
    all_to_all x1, blocking collectives, per_device(): lax.all_to_all(far, ('mp', 'example', 'layer'), split_axis=0, concat_axis...  63.4 us
    all_gather x1, waiting for transfers between devices, per_device(): near = lax.all_gather(near, 'mp', axis=0, tiled=True)  33.9 us
    pallas_call x2, Pallas kernels, _up_project(): pl.pallas_call(kernel, grid=(shares // per_tile,), in_specs=[pl.BlockSpec...  32.9 us
    all_to_all x1, blocking collectives, per_device(): lax.all_to_all(near, ('layer', 'example'), split_axis=0, concat_axis=0, t...  16.7 us
    all_to_all x1, waiting for transfers between devices, per_device(): lax.all_to_all(jnp.broadcast_to(projected, (doc_devices, projected.shape[...  12.2 us
    all_to_all x1, waiting for transfers between devices, per_device(): lax.all_to_all(out_part.reshape(doc_devices, own_rows, out_width), ('mp',...  11.1 us
    unnamed x14, local copies, waits for them, and re-layouts  4.87 us
    dot_general x1, matrix products, per_device(): lax.dot_general(col_block, all_docs, (((0,), (0,)), ((), ())), precision=...  4.83 us
  transfers between devices with their start and end apart: 4, of which 4 were waited for; matrix products, arithmetic and copies ran while one was open for 3% of the time, Pallas kernels for 8%

profile of v5, /device:TPU:0, one launch (start us, length us, event | category | flops | bytes accessed | tf_op | source)
XLA Modules:
  0.0 216.0 jit_solution(16486111581693007308)
XLA Ops:
  7.2 0.0 copy-start
  7.2 0.0 all-gather.2.cloned.1.call-start
  7.2 1.2 fusion.12
  8.4 0.0 slice-start
  8.5 16.7 %all_to_all.29 = bf16[16,8,2048]{2,1,0:T(8,128)(2,1)} all-to-all(bf16[16,8,2048]{2,1,0:T(8,128)(2,1)S(1)} %bitcast.53), channel_id=1, replica_groups=mesh['mp'=8,'layer'=4,'example'=4] {'layer','example'}, dimensions={0} | all-to-all | bytes 1048576 | tf_op jit(solution)/shard_map/all_to_all | solution.py:77
  25.2 0.0 all-gather.2.cloned.1.call-update
  25.3 0.0 slice-done
  25.3 0.5 broadcast_in_dim.8
  25.8 0.0 copy-start.2
  25.9 63.4 %all_to_all.30 = bf16[128,8,2048]{2,1,0:T(8,128)(2,1)S(1)} all-to-all(bf16[128,8,2048]{2,1,0:T(8,128)(2,1)S(1)} %bitcast.51), channel_id=1, replica_groups=mesh['mp'=8,'layer'=4,'example'=4] {'mp','example','layer'}, dimensions={0} | all-to-all | bytes 8388608 | tf_op jit(solution)/shard_map/all_to_all | solution.py:85
  89.3 0.0 copy-done.2
  89.3 16.5 %shard_map.105 = f32[1024,64]{1,0:T(8,128)S(1)} custom-call(bf16[1024,2048]{1,0:T(8,128)(2,1)S(1)} %bitcast.41, bf16[1792,2048]{1,0:T(8,128)(2,1)} %bitcast.47, bf16[8,4,4,16,1792]{4,3,2,1,0:T(8,128)(2,1)} %bitcast.49, bf16[64,1792]{1,0:T(8,128)(2,1)S(1)} %bitcast.45), custom_call_target="tpu_custom_call" | custom-call | tf_op jit(solution)/shard_map/pallas_call | solution.py:41
  105.8 0.1 copy.33
  105.8 33.9 %all-gather.2.cloned.1.call-done = bf16[128,8,2048]{2,1,0:T(8,128)(2,1)} async-done(((bf16[16,8,2048]{2,1,0:T(8,128)(2,1)}), bf16[128,8,2048]{2,1,0:T(8,128)(2,1)}) %all-gather.2.cloned.1.call-update) | async-done | bytes 4194320 | tf_op jit(solution)/shard_map/all_gather | solution.py:78
  139.7 0.0 copy-start.1
  139.7 2.2 %copy-done.1 = bf16[128,8,2048]{2,1,0:T(8,128)(2,1)S(1)} copy-done((bf16[128,8,2048]{2,1,0:T(8,128)(2,1)S(1)}, bf16[128,8,2048]{2,1,0:T(8,128)(2,1)}, u32[]{:S(2)}) %copy-start.1) | copy-done | bytes 4194328
  141.9 16.4 %shard_map.104 = f32[1024,64]{1,0:T(8,128)S(1)} custom-call(bf16[1024,2048]{1,0:T(8,128)(2,1)S(1)} %bitcast.42, bf16[1792,2048]{1,0:T(8,128)(2,1)} %bitcast.48, bf16[8,4,4,16,1792]{4,3,2,1,0:T(8,128)(2,1)} %bitcast.50, bf16[64,1792]{1,0:T(8,128)(2,1)S(1)} %bitcast.46), custom_call_target="tpu_custom_call" | custom-call | tf_op jit(solution)/shard_map/pallas_call | solution.py:41
  158.4 0.1 pad_maximum_fusion
  158.5 0.0 copy-start.3
  158.5 1.4 reshape.89
  159.9 3.9 %all-to-all-start.2 = ((f32[32,1,4096]{2,1,0:T(1,128)}), f32[32,1,4096]{2,1,0:T(1,128)S(1)}, u32[]{:S(2)}, u32[]{:S(2)}) async-start(f32[32,1,4096]{2,1,0:T(1,128)} %reshape.89), calls=%async_computation.2 | async-start | bytes 1048576 | tf_op jit(solution)/shard_map/all_to_all | solution.py:98
  164.5 0.0 copy-done
  164.5 0.0 copy-done.3
  164.5 0.4 fusion.2
  164.9 11.1 %all-to-all-done.2 = f32[32,1,4096]{2,1,0:T(1,128)S(1)} async-done(((f32[32,1,4096]{2,1,0:T(1,128)}), f32[32,1,4096]{2,1,0:T(1,128)S(1)}, u32[]{:S(2)}, u32[]{:S(2)}) %all-to-all-start.2) | async-done | bytes 524320 | tf_op jit(solution)/shard_map/all_to_all | solution.py:98
  176.1 0.5 broadcast.31
  176.6 1.8 reduce
  178.4 0.0 copy-start.4
  178.4 0.4 reshape.90
  178.8 0.1 reduce_sum.18
  178.9 0.3 convolution_multiply_fusion.1
  179.2 0.1 mul.39
  179.3 1.3 broadcast_in_dim.9
  180.6 3.9 %all-to-all-start.3 = ((f32[32,1,4096]{2,1,0:T(1,128)}), f32[32,1,4096]{2,1,0:T(1,128)S(1)}, u32[]{:S(2)}, u32[]{:S(2)}) async-start(f32[32,1,4096]{2,1,0:T(1,128)} %broadcast_in_dim.9), calls=%async_computation.3 | async-start | bytes 1048576 | tf_op jit(solution)/shard_map/all_to_all | solution.py:123
  184.5 12.2 %all-to-all-done.3 = f32[32,1,4096]{2,1,0:T(1,128)S(1)} async-done(((f32[32,1,4096]{2,1,0:T(1,128)}), f32[32,1,4096]{2,1,0:T(1,128)S(1)}, u32[]{:S(2)}, u32[]{:S(2)}) %all-to-all-start.3) | async-done | bytes 524320 | tf_op jit(solution)/shard_map/all_to_all | solution.py:123
  196.7 0.0 copy-done.4
  196.7 0.7 convolution_bitcast_fusion
  197.4 0.1 copy.22
  197.5 0.7 reshape.91
  198.2 4.3 %all-to-all-start.4 = ((f32[4,1,1024]{2,1,0:T(1,128)}), f32[4,1,1024]{2,1,0:T(1,128)S(1)}, u32[]{:S(2)}, u32[]{:S(2)}) async-start(f32[4,1,1024]{2,1,0:T(1,128)} %reshape.91), calls=%async_computation.4 | async-start | bytes 32768 | tf_op jit(solution)/shard_map/all_to_all | solution.py:146
  202.5 4.8 %fusion.1 = f32[1,128,4096]{2,1,0:T(8,128)} fusion(f32[32,128]{1,0:T(8,128)S(1)} %bitcast.56, f32[1,128,4096]{2,1,0:T(8,128)} %param.16, f32[32,1,4096]{2,1,0:T(1,128)S(1)} %all-to-all-done.3), kind=kOutput, calls=%fused_computation.2 | convolution fusion | flops 202375168 | bytes 4734976 | tf_op jit(solution)/shard_map/dot_general | solution.py:134
  207.3 0.5 all-to-all-done.4
  207.8 0.6 reduce.1
  208.4 0.1 reshape.92
  208.5 0.6 reduce_sum.19
  (5 shorter events, 0.1 us)
Async XLA Ops:
  7.2 157.3 %copy-start = (bf16[1,64,8192]{2,1,0:T(8,128)(2,1)S(1)}, bf16[1,64,8192]{2,1,0:T(8,128)(2,1)}, u32[]{:S(2)}) copy-start(bf16[1,64,8192]{2,1,0:T(8,128)(2,1)} %param.14) | copy-start | bytes 3145732
  7.2 132.6 %all-gather.2.cloned.1.call-start = ((), (), s32[]{:S(2)}) async-start(), calls=%async_computation.5 | async-start | bytes 4718592 | tf_op jit(solution)/shard_map/all_gather | solution.py:78
  8.4 16.8 %slice-start = ((bf16[4,16,8192]{2,1,0:T(8,128)(2,1)}), bf16[4,8,8192]{2,1,0:T(8,128)(2,1)S(1)}, s32[]{:S(2)}) async-start(bf16[4,16,8192]{2,1,0:T(8,128)(2,1)} %param.9), calls=%async_computation.6 | async-start | bytes 1048576 | tf_op jit(solution)/shard_map/slice | solution.py:80
  25.8 63.5 %copy-start.2 = (bf16[1,64,1792]{2,1,0:T(8,128)(2,1)S(1)}, bf16[1,64,1792]{2,1,0:T(8,128)(2,1)}, u32[]{:S(2)}) copy-start(bf16[1,64,1792]{2,1,0:T(8,128)(2,1)} %param.13) | copy-start | bytes 688132
  139.7 2.2 %copy-start.1 = (bf16[128,8,2048]{2,1,0:T(8,128)(2,1)S(1)}, bf16[128,8,2048]{2,1,0:T(8,128)(2,1)}, u32[]{:S(2)}) copy-start(bf16[128,8,2048]{2,1,0:T(8,128)(2,1)} %all-gather.2.cloned.1.call-done) | copy-start | bytes 12582916
  158.5 6.0 %copy-start.3 = (bf16[1,64,8192]{2,1,0:T(8,128)(2,1)S(1)}, bf16[1,64,8192]{2,1,0:T(8,128)(2,1)}, u32[]{:S(2)}) copy-start(bf16[1,64,8192]{2,1,0:T(8,128)(2,1)} %param.12) | copy-start | bytes 3145732
  159.9 16.1 %all-to-all-start.2 = ((f32[32,1,4096]{2,1,0:T(1,128)}), f32[32,1,4096]{2,1,0:T(1,128)S(1)}, u32[]{:S(2)}, u32[]{:S(2)}) async-start(f32[32,1,4096]{2,1,0:T(1,128)} %reshape.89), calls=%async_computation.2 | async-start | bytes 1048576 | tf_op jit(solution)/shard_map/all_to_all | solution.py:98
  178.4 18.3 %copy-start.4 = (bf16[1,32,4096]{2,1,0:T(8,128)(2,1)S(1)}, bf16[1,32,4096]{2,1,0:T(8,128)(2,1)}, u32[]{:S(2)}) copy-start(bf16[1,32,4096]{2,1,0:T(8,128)(2,1)} %param.15) | copy-start | bytes 786436
  180.6 16.1 %all-to-all-start.3 = ((f32[32,1,4096]{2,1,0:T(1,128)}), f32[32,1,4096]{2,1,0:T(1,128)S(1)}, u32[]{:S(2)}, u32[]{:S(2)}) async-start(f32[32,1,4096]{2,1,0:T(1,128)} %broadcast_in_dim.9), calls=%async_computation.3 | async-start | bytes 1048576 | tf_op jit(solution)/shard_map/all_to_all | solution.py:123
  198.2 9.7 %all-to-all-start.4 = ((f32[4,1,1024]{2,1,0:T(1,128)}), f32[4,1,1024]{2,1,0:T(1,128)S(1)}, u32[]{:S(2)}, u32[]{:S(2)}) async-start(f32[4,1,1024]{2,1,0:T(1,128)} %reshape.91), calls=%async_computation.4 | async-start | bytes 32768 | tf_op jit(solution)/shard_map/all_to_all | solution.py:146
Sparse Core Ops, SparseCore 0:
  25.4 114.3 all-gather.1

commit v6 on v4

--- a/solution.py
+++ b/solution.py
@@ -19,9 +19,18 @@
     low = (scaled - high.astype(jnp.float32)).astype(jnp.bfloat16)
     proj = proj_ref[...]
     dims = (((1,), (1,)), ((), ()))
-    out_ref[...] = lax.dot_general(
+    result = lax.dot_general(
         high, proj, dims, preferred_element_type=jnp.float32
     ) + lax.dot_general(low, proj, dims, preferred_element_type=jnp.float32)
+    rows = gate_ref.shape[3]
+    out_ref[...] = jnp.concatenate(
+        [
+            result[(e * layers + l) * rows : (e * layers + l + 1) * rows]
+            for l in range(layers)
+            for e in range(groups)
+        ],
+        axis=0,
+    )
 
 
 def _up_project(token_cols, weight, gate5, proj):
@@ -73,9 +82,6 @@
     own_rows = layer_input.shape[1]
     gate5 = gate_act[0].reshape(shares, layer_count, groups, local_rows, gate_act.shape[2])
     out_part = _up_project(token_cols, down_weight[0], gate5, proj_out[0])
-    out_part = jnp.transpose(
-        out_part.reshape(shares, groups, layer_count, local_rows, out_width), (0, 2, 1, 3, 4)
-    ).reshape(-1, out_width)
     doc_devices = lax.axis_size(("mp", "example"))
     gathered = lax.all_to_all(
         out_part.reshape(doc_devices, own_rows, out_width),

time: 193 us -> 193 us (level)
  no operation moved by 1% of the time
where the time goes in v6:
time: 193 us; the launch traced here: 192 us
  blocking collectives  108 us (56%)
  Pallas kernels  29.3 us (15%)
  waiting for transfers between devices  23.9 us (12%)
  starting transfers between devices  12.1 us (6%)
  local copies, waits for them, and re-layouts  8.27 us (4%)
  matrix products  6.21 us (3%)
  other arithmetic  3.38 us (2%)
    all_to_all x1, blocking collectives, per_device(): lax.all_to_all(pieces, ('mp', 'example', 'layer'), split_axis=0, concat_a...  108 us
    pallas_call x1, Pallas kernels, _up_project(): pl.pallas_call(_up_kernel, grid=(blocks,), in_specs=[pl.BlockSpec((tile,...  29.3 us
    all_to_all x1, waiting for transfers between devices, per_device(): lax.all_to_all(jnp.broadcast_to(projected, (doc_devices, projected.shape[...  12.2 us
    all_to_all x1, waiting for transfers between devices, per_device(): lax.all_to_all(out_part.reshape(doc_devices, own_rows, out_width), ('mp',...  11.1 us
    dot_general x1, matrix products, per_device(): lax.dot_general(col_block, all_docs, (((0,), (0,)), ((), ())), precision=...  4.83 us
    all_to_all x1, starting transfers between devices, per_device(): lax.all_to_all(out_part.reshape(doc_devices, own_rows, out_width), ('mp',...  4.19 us
    all_to_all x1, starting transfers between devices, per_device(): lax.all_to_all(jnp.broadcast_to(score_part[None], (layers,) + score_part....  4.05 us
    all_to_all x1, starting transfers between devices, per_device(): lax.all_to_all(jnp.broadcast_to(projected, (doc_devices, projected.shape[...  3.89 us
  transfers between devices with their start and end apart: 3, of which 3 were waited for; matrix products, arithmetic and copies ran while one was open for 3% of the time, Pallas kernels for 0%

profile of v6, /device:TPU:0, one launch (start us, length us, event | category | flops | bytes accessed | tf_op | source)
XLA Modules:
  0.0 192.5 jit_solution(4517096200484690370)
XLA Ops:
  0.6 0.0 copy-start
  0.6 1.9 %reshape.72 = bf16[4,16,4,2048]{3,2,1,0:T(4,128)(2,1)S(1)} reshape(bf16[4,16,8192]{2,1,0:T(8,128)(2,1)} %param.9) | data formatting | bytes 2097152 | tf_op jit(solution)/shard_map/reshape | solution.py:72
  2.6 0.6 copy.13
  3.2 1.1 broadcast_in_dim.8
  4.2 0.0 copy-start.1
  4.2 107.9 %all_to_all.24 = bf16[128,16,2048]{2,1,0:T(8,128)(2,1)} all-to-all(bf16[128,16,2048]{2,1,0:T(8,128)(2,1)S(1)} %bitcast.34), channel_id=1, replica_groups=mesh['mp'=8,'layer'=4,'example'=4] {'mp','example','layer'}, dimensions={0} | all-to-all | bytes 16777216 | tf_op jit(solution)/shard_map/all_to_all | solution.py:77
  112.1 0.0 copy-done.1
  112.1 29.3 %shard_map.104 = f32[2048,64]{1,0:T(8,128)S(1)} custom-call(bf16[2048,2048]{1,0:T(8,128)(2,1)} %bitcast.35, bf16[1792,2048]{1,0:T(8,128)(2,1)} %bitcast.36, bf16[8,4,4,16,1792]{4,3,2,1,0:T(8,128)(2,1)} %bitcast.37, bf16[64,1792]{1,0:T(8,128)(2,1)S(1)} %bitcast.33), custom_call_target="tpu_custom_call" | custom-call | tf_op jit(solution)/shard_map/pallas_call | solution.py:42
  141.4 0.0 copy-start.2
  141.4 1.4 reshape.76
  142.8 4.2 %all-to-all-start.1 = ((f32[32,1,4096]{2,1,0:T(1,128)}), f32[32,1,4096]{2,1,0:T(1,128)S(1)}, u32[]{:S(2)}, u32[]{:S(2)}) async-start(f32[32,1,4096]{2,1,0:T(1,128)} %reshape.76), calls=%async_computation.1 | async-start | bytes 1048576 | tf_op jit(solution)/shard_map/all_to_all | solution.py:86
  147.7 0.0 copy-done
  147.7 0.0 copy-done.2
  147.7 0.4 fusion.2
  148.1 11.1 %all-to-all-done.1 = f32[32,1,4096]{2,1,0:T(1,128)S(1)} async-done(((f32[32,1,4096]{2,1,0:T(1,128)}), f32[32,1,4096]{2,1,0:T(1,128)S(1)}, u32[]{:S(2)}, u32[]{:S(2)}) %all-to-all-start.1) | async-done | bytes 524320 | tf_op jit(solution)/shard_map/all_to_all | solution.py:86
  159.3 0.6 broadcast.31
  159.9 1.9 %reduce = f32[32,4096]{1,0:T(8,128)S(1)} reduce(f32[32,1,4096]{2,1,0:T(1,128)S(1)} %all-to-all-done.1, f32[]{:T(128)} %broadcast.31), dimensions={1}, to_apply=%all_to_all.16.reduce_sub_computation | reduce | bytes 1048580 | tf_op jit(solution)/shard_map/all_to_all | solution.py:86
  161.8 0.0 copy-start.3
  161.8 0.4 reshape.77
  162.3 0.1 reduce_sum.18
  162.3 0.3 convolution_multiply_fusion.1
  162.7 0.1 mul.39
  162.7 1.3 broadcast_in_dim.9
  164.0 3.9 %all-to-all-start.2 = ((f32[32,1,4096]{2,1,0:T(1,128)}), f32[32,1,4096]{2,1,0:T(1,128)S(1)}, u32[]{:S(2)}, u32[]{:S(2)}) async-start(f32[32,1,4096]{2,1,0:T(1,128)} %broadcast_in_dim.9), calls=%async_computation.2 | async-start | bytes 1048576 | tf_op jit(solution)/shard_map/all_to_all | solution.py:111
  167.9 12.2 %all-to-all-done.2 = f32[32,1,4096]{2,1,0:T(1,128)S(1)} async-done(((f32[32,1,4096]{2,1,0:T(1,128)}), f32[32,1,4096]{2,1,0:T(1,128)S(1)}, u32[]{:S(2)}, u32[]{:S(2)}) %all-to-all-start.2) | async-done | bytes 524320 | tf_op jit(solution)/shard_map/all_to_all | solution.py:111
  180.2 0.0 copy-done.3
  180.2 0.7 convolution_bitcast_fusion
  180.8 0.1 copy.14
  180.9 0.7 reshape.78
  181.6 4.1 %all-to-all-start.3 = ((f32[4,1,1024]{2,1,0:T(1,128)}), f32[4,1,1024]{2,1,0:T(1,128)S(1)}, u32[]{:S(2)}, u32[]{:S(2)}) async-start(f32[4,1,1024]{2,1,0:T(1,128)} %reshape.78), calls=%async_computation.3 | async-start | bytes 32768 | tf_op jit(solution)/shard_map/all_to_all | solution.py:134
  185.7 4.8 %fusion.1 = f32[1,128,4096]{2,1,0:T(8,128)} fusion(f32[32,128]{1,0:T(8,128)S(1)} %bitcast.39, f32[1,128,4096]{2,1,0:T(8,128)} %param.16, f32[32,1,4096]{2,1,0:T(1,128)S(1)} %all-to-all-done.2), kind=kOutput, calls=%fused_computation.2 | convolution fusion | flops 202375168 | bytes 4734976 | tf_op jit(solution)/shard_map/dot_general | solution.py:122
  190.5 0.5 all-to-all-done.3
  191.0 0.7 reduce.1
  191.8 0.1 reshape.79
  191.9 0.6 reduce_sum.19
  (3 shorter events, 0.0 us)
Async XLA Ops:
  0.6 147.1 %copy-start = (bf16[1,64,8192]{2,1,0:T(8,128)(2,1)S(1)}, bf16[1,64,8192]{2,1,0:T(8,128)(2,1)}, u32[]{:S(2)}) copy-start(bf16[1,64,8192]{2,1,0:T(8,128)(2,1)} %param.14) | copy-start | bytes 3145732
  4.2 107.9 %copy-start.1 = (bf16[1,64,1792]{2,1,0:T(8,128)(2,1)S(1)}, bf16[1,64,1792]{2,1,0:T(8,128)(2,1)}, u32[]{:S(2)}) copy-start(bf16[1,64,1792]{2,1,0:T(8,128)(2,1)} %param.13) | copy-start | bytes 688132
  141.4 6.3 %copy-start.2 = (bf16[1,64,8192]{2,1,0:T(8,128)(2,1)S(1)}, bf16[1,64,8192]{2,1,0:T(8,128)(2,1)}, u32[]{:S(2)}) copy-start(bf16[1,64,8192]{2,1,0:T(8,128)(2,1)} %param.12) | copy-start | bytes 3145732
  142.8 16.4 %all-to-all-start.1 = ((f32[32,1,4096]{2,1,0:T(1,128)}), f32[32,1,4096]{2,1,0:T(1,128)S(1)}, u32[]{:S(2)}, u32[]{:S(2)}) async-start(f32[32,1,4096]{2,1,0:T(1,128)} %reshape.76), calls=%async_computation.1 | async-start | bytes 1048576 | tf_op jit(solution)/shard_map/all_to_all | solution.py:86
  161.8 18.3 %copy-start.3 = (bf16[1,32,4096]{2,1,0:T(8,128)(2,1)S(1)}, bf16[1,32,4096]{2,1,0:T(8,128)(2,1)}, u32[]{:S(2)}) copy-start(bf16[1,32,4096]{2,1,0:T(8,128)(2,1)} %param.15) | copy-start | bytes 786436
  164.0 16.2 %all-to-all-start.2 = ((f32[32,1,4096]{2,1,0:T(1,128)}), f32[32,1,4096]{2,1,0:T(1,128)S(1)}, u32[]{:S(2)}, u32[]{:S(2)}) async-start(f32[32,1,4096]{2,1,0:T(1,128)} %broadcast_in_dim.9), calls=%async_computation.2 | async-start | bytes 1048576 | tf_op jit(solution)/shard_map/all_to_all | solution.py:111
  181.6 9.4 %all-to-all-start.3 = ((f32[4,1,1024]{2,1,0:T(1,128)}), f32[4,1,1024]{2,1,0:T(1,128)S(1)}, u32[]{:S(2)}, u32[]{:S(2)}) async-start(f32[4,1,1024]{2,1,0:T(1,128)} %reshape.78), calls=%async_computation.3 | async-start | bytes 32768 | tf_op jit(solution)/shard_map/all_to_all | solution.py:134

commit v7 on v6

--- a/solution.py
+++ b/solution.py
@@ -10,9 +10,15 @@
     hidden = lax.dot_general(
         cot_ref[...], w_ref[...], (((1,), (1,)), ((), ())), preferred_element_type=jnp.float32
     )
-    layers, groups = gate_ref.shape[1], gate_ref.shape[2]
+    blocks, layers, groups = gate_ref.shape[:3]
     gate = jnp.concatenate(
-        [gate_ref[0, l, e] for e in range(groups) for l in range(layers)], axis=0
+        [
+            gate_ref[b, l, e]
+            for b in range(blocks)
+            for e in range(groups)
+            for l in range(layers)
+        ],
+        axis=0,
     ).astype(jnp.float32)
     scaled = hidden * gate
     high = scaled.astype(jnp.bfloat16)
@@ -25,7 +31,8 @@
     rows = gate_ref.shape[3]
     out_ref[...] = jnp.concatenate(
         [
-            result[(e * layers + l) * rows : (e * layers + l + 1) * rows]
+            result[((b * groups + e) * layers + l) * rows :][:rows]
+            for b in range(blocks)
             for l in range(layers)
             for e in range(groups)
         ],
@@ -37,7 +44,9 @@
     tokens, feats = token_cols.shape
     hidden = weight.shape[0]
     width = proj.shape[0]
-    blocks, layers, groups, rows = gate5.shape[:4]
+    shares, layers, groups, rows = gate5.shape[:4]
+    per_tile = 2
+    blocks = shares // per_tile
     tile = tokens // blocks
     return pl.pallas_call(
         _up_kernel,
@@ -45,7 +54,7 @@
         in_specs=[
             pl.BlockSpec((tile, feats), lambda i: (i, 0)),
             pl.BlockSpec((hidden, feats), lambda i: (0, 0)),
-            pl.BlockSpec((1, layers, groups, rows, hidden), lambda i: (i, 0, 0, 0, 0)),
+            pl.BlockSpec((per_tile, layers, groups, rows, hidden), lambda i: (i, 0, 0, 0, 0)),
             pl.BlockSpec((width, hidden), lambda i: (0, 0)),
         ],
         out_specs=pl.BlockSpec((tile, width), lambda i: (i, 0)),

time: 193 us -> 192 us (level)
  no operation moved by 1% of the time
where the time goes in v7:
time: 192 us
  blocking collectives  108 us (56%)
  Pallas kernels  28.4 us (15%)
  waiting for transfers between devices  23.9 us (12%)
  starting transfers between devices  12.1 us (6%)
  local copies, waits for them, and re-layouts  8.27 us (4%)
  matrix products  6.21 us (3%)
  other arithmetic  3.38 us (2%)
    all_to_all x1, blocking collectives, per_device(): lax.all_to_all(pieces, ('mp', 'example', 'layer'), split_axis=0, concat_a...  108 us
    pallas_call x1, Pallas kernels, _up_project(): pl.pallas_call(_up_kernel, grid=(blocks,), in_specs=[pl.BlockSpec((tile,...  28.4 us
    all_to_all x1, waiting for transfers between devices, per_device(): lax.all_to_all(jnp.broadcast_to(projected, (doc_devices, projected.shape[...  12.2 us
    all_to_all x1, waiting for transfers between devices, per_device(): lax.all_to_all(out_part.reshape(doc_devices, own_rows, out_width), ('mp',...  11.1 us
    dot_general x1, matrix products, per_device(): lax.dot_general(col_block, all_docs, (((0,), (0,)), ((), ())), precision=...  4.83 us
    all_to_all x1, starting transfers between devices, per_device(): lax.all_to_all(out_part.reshape(doc_devices, own_rows, out_width), ('mp',...  4.19 us
    all_to_all x1, starting transfers between devices, per_device(): lax.all_to_all(jnp.broadcast_to(score_part[None], (layers,) + score_part....  4.05 us
    all_to_all x1, starting transfers between devices, per_device(): lax.all_to_all(jnp.broadcast_to(projected, (doc_devices, projected.shape[...  3.89 us
  transfers between devices with their start and end apart: 3, of which 3 were waited for; matrix products, arithmetic and copies ran while one was open for 3% of the time, Pallas kernels for 0%

profile of v7, /device:TPU:0, one launch (start us, length us, event | category | flops | bytes accessed | tf_op | source)
XLA Modules:
  0.0 191.6 jit_solution(14422107835557223183)
XLA Ops:
  0.6 0.0 copy-start
  0.6 1.9 %reshape.72 = bf16[4,16,4,2048]{3,2,1,0:T(4,128)(2,1)S(1)} reshape(bf16[4,16,8192]{2,1,0:T(8,128)(2,1)} %param.9) | data formatting | bytes 2097152 | tf_op jit(solution)/shard_map/reshape | solution.py:81
  2.6 0.6 copy.13
  3.2 1.1 broadcast_in_dim.8
  4.2 0.0 copy-start.1
  4.2 107.9 %all_to_all.24 = bf16[128,16,2048]{2,1,0:T(8,128)(2,1)} all-to-all(bf16[128,16,2048]{2,1,0:T(8,128)(2,1)S(1)} %bitcast.34), channel_id=1, replica_groups=mesh['mp'=8,'layer'=4,'example'=4] {'mp','example','layer'}, dimensions={0} | all-to-all | bytes 16777216 | tf_op jit(solution)/shard_map/all_to_all | solution.py:86
  112.1 0.0 copy-done.1
  112.1 28.4 %shard_map.104 = f32[2048,64]{1,0:T(8,128)S(1)} custom-call(bf16[2048,2048]{1,0:T(8,128)(2,1)} %bitcast.35, bf16[1792,2048]{1,0:T(8,128)(2,1)} %bitcast.36, bf16[8,4,4,16,1792]{4,3,2,1,0:T(8,128)(2,1)} %bitcast.37, bf16[64,1792]{1,0:T(8,128)(2,1)S(1)} %bitcast.33), custom_call_target="tpu_custom_call" | custom-call | tf_op jit(solution)/shard_map/pallas_call | solution.py:51
  140.5 0.0 copy-start.2
  140.5 1.4 reshape.76
  141.9 4.2 %all-to-all-start.1 = ((f32[32,1,4096]{2,1,0:T(1,128)}), f32[32,1,4096]{2,1,0:T(1,128)S(1)}, u32[]{:S(2)}, u32[]{:S(2)}) async-start(f32[32,1,4096]{2,1,0:T(1,128)} %reshape.76), calls=%async_computation.1 | async-start | bytes 1048576 | tf_op jit(solution)/shard_map/all_to_all | solution.py:95
  146.8 0.0 copy-done
  146.8 0.0 copy-done.2
  146.8 0.4 fusion.2
  147.2 11.1 %all-to-all-done.1 = f32[32,1,4096]{2,1,0:T(1,128)S(1)} async-done(((f32[32,1,4096]{2,1,0:T(1,128)}), f32[32,1,4096]{2,1,0:T(1,128)S(1)}, u32[]{:S(2)}, u32[]{:S(2)}) %all-to-all-start.1) | async-done | bytes 524320 | tf_op jit(solution)/shard_map/all_to_all | solution.py:95
  158.4 0.6 broadcast.31
  159.0 1.9 %reduce = f32[32,4096]{1,0:T(8,128)S(1)} reduce(f32[32,1,4096]{2,1,0:T(1,128)S(1)} %all-to-all-done.1, f32[]{:T(128)} %broadcast.31), dimensions={1}, to_apply=%all_to_all.16.reduce_sub_computation | reduce | bytes 1048580 | tf_op jit(solution)/shard_map/all_to_all | solution.py:95
  160.9 0.0 copy-start.3
  160.9 0.4 reshape.77
  161.4 0.1 reduce_sum.18
  161.5 0.3 convolution_multiply_fusion.1
  161.8 0.1 mul.39
  161.8 1.3 broadcast_in_dim.9
  163.1 3.9 %all-to-all-start.2 = ((f32[32,1,4096]{2,1,0:T(1,128)}), f32[32,1,4096]{2,1,0:T(1,128)S(1)}, u32[]{:S(2)}, u32[]{:S(2)}) async-start(f32[32,1,4096]{2,1,0:T(1,128)} %broadcast_in_dim.9), calls=%async_computation.2 | async-start | bytes 1048576 | tf_op jit(solution)/shard_map/all_to_all | solution.py:120
  167.0 12.2 %all-to-all-done.2 = f32[32,1,4096]{2,1,0:T(1,128)S(1)} async-done(((f32[32,1,4096]{2,1,0:T(1,128)}), f32[32,1,4096]{2,1,0:T(1,128)S(1)}, u32[]{:S(2)}, u32[]{:S(2)}) %all-to-all-start.2) | async-done | bytes 524320 | tf_op jit(solution)/shard_map/all_to_all | solution.py:120
  179.3 0.0 copy-done.3
  179.3 0.7 convolution_bitcast_fusion
  179.9 0.1 copy.14
  180.0 0.7 reshape.78
  180.7 4.1 %all-to-all-start.3 = ((f32[4,1,1024]{2,1,0:T(1,128)}), f32[4,1,1024]{2,1,0:T(1,128)S(1)}, u32[]{:S(2)}, u32[]{:S(2)}) async-start(f32[4,1,1024]{2,1,0:T(1,128)} %reshape.78), calls=%async_computation.3 | async-start | bytes 32768 | tf_op jit(solution)/shard_map/all_to_all | solution.py:143
  184.8 4.8 %fusion.1 = f32[1,128,4096]{2,1,0:T(8,128)} fusion(f32[32,128]{1,0:T(8,128)S(1)} %bitcast.39, f32[1,128,4096]{2,1,0:T(8,128)} %param.16, f32[32,1,4096]{2,1,0:T(1,128)S(1)} %all-to-all-done.2), kind=kOutput, calls=%fused_computation.2 | convolution fusion | flops 202375168 | bytes 4734976 | tf_op jit(solution)/shard_map/dot_general | solution.py:131
  189.6 0.5 all-to-all-done.3
  190.1 0.7 reduce.1
  190.9 0.1 reshape.79
  191.0 0.6 reduce_sum.19
  (3 shorter events, 0.0 us)
Async XLA Ops:
  0.6 146.2 %copy-start = (bf16[1,64,8192]{2,1,0:T(8,128)(2,1)S(1)}, bf16[1,64,8192]{2,1,0:T(8,128)(2,1)}, u32[]{:S(2)}) copy-start(bf16[1,64,8192]{2,1,0:T(8,128)(2,1)} %param.14) | copy-start | bytes 3145732
  4.2 107.9 %copy-start.1 = (bf16[1,64,1792]{2,1,0:T(8,128)(2,1)S(1)}, bf16[1,64,1792]{2,1,0:T(8,128)(2,1)}, u32[]{:S(2)}) copy-start(bf16[1,64,1792]{2,1,0:T(8,128)(2,1)} %param.13) | copy-start | bytes 688132
  140.5 6.3 %copy-start.2 = (bf16[1,64,8192]{2,1,0:T(8,128)(2,1)S(1)}, bf16[1,64,8192]{2,1,0:T(8,128)(2,1)}, u32[]{:S(2)}) copy-start(bf16[1,64,8192]{2,1,0:T(8,128)(2,1)} %param.12) | copy-start | bytes 3145732
  141.9 16.4 %all-to-all-start.1 = ((f32[32,1,4096]{2,1,0:T(1,128)}), f32[32,1,4096]{2,1,0:T(1,128)S(1)}, u32[]{:S(2)}, u32[]{:S(2)}) async-start(f32[32,1,4096]{2,1,0:T(1,128)} %reshape.76), calls=%async_computation.1 | async-start | bytes 1048576 | tf_op jit(solution)/shard_map/all_to_all | solution.py:95
  160.9 18.3 %copy-start.3 = (bf16[1,32,4096]{2,1,0:T(8,128)(2,1)S(1)}, bf16[1,32,4096]{2,1,0:T(8,128)(2,1)}, u32[]{:S(2)}) copy-start(bf16[1,32,4096]{2,1,0:T(8,128)(2,1)} %param.15) | copy-start | bytes 786436
  163.1 16.2 %all-to-all-start.2 = ((f32[32,1,4096]{2,1,0:T(1,128)}), f32[32,1,4096]{2,1,0:T(1,128)S(1)}, u32[]{:S(2)}, u32[]{:S(2)}) async-start(f32[32,1,4096]{2,1,0:T(1,128)} %broadcast_in_dim.9), calls=%async_computation.2 | async-start | bytes 1048576 | tf_op jit(solution)/shard_map/all_to_all | solution.py:120
  180.7 9.4 %all-to-all-start.3 = ((f32[4,1,1024]{2,1,0:T(1,128)}), f32[4,1,1024]{2,1,0:T(1,128)S(1)}, u32[]{:S(2)}, u32[]{:S(2)}) async-start(f32[4,1,1024]{2,1,0:T(1,128)} %reshape.78), calls=%async_computation.3 | async-start | bytes 32768 | tf_op jit(solution)/shard_map/all_to_all | solution.py:143

commit v8 on v7

--- a/solution.py
+++ b/solution.py
@@ -78,8 +78,9 @@
     groups = lax.axis_size("example")
     shares = lax.axis_size("mp")
     col_width = model_width // groups
-    pieces = cotangent.reshape(layer_count, local_rows, groups, col_width)
-    pieces = jnp.transpose(pieces, (2, 0, 1, 3))
+    pieces = jnp.stack(
+        [cotangent[:, :, e * col_width : (e + 1) * col_width] for e in range(groups)]
+    )
     pieces = jnp.broadcast_to(pieces[None], (shares,) + pieces.shape).reshape(
         shares * groups * layer_count, local_rows, col_width
     )

time: 192 us -> 191 us (level)
    reshape x1 -> x0, local copies, waits for them, and re-layouts: 1.93 us -> none  [per_device(): pieces = cotangent.reshape(layer_count, local_rows, groups, col_width)]
where the time goes in v8:
time: 191 us
  blocking collectives  108 us (57%)
  Pallas kernels  28.4 us (15%)
  waiting for transfers between devices  23.9 us (13%)
  starting transfers between devices  12.1 us (6%)
  local copies, waits for them, and re-layouts  7.1 us (4%)
  matrix products  6.21 us (3%)
  other arithmetic  3.52 us (2%)
    all_to_all x1, blocking collectives, per_device(): lax.all_to_all(pieces, ('mp', 'example', 'layer'), split_axis=0, concat_a...  108 us
    pallas_call x1, Pallas kernels, _up_project(): pl.pallas_call(_up_kernel, grid=(blocks,), in_specs=[pl.BlockSpec((tile,...  28.4 us
    all_to_all x1, waiting for transfers between devices, per_device(): lax.all_to_all(jnp.broadcast_to(projected, (doc_devices, projected.shape[...  12.2 us
    all_to_all x1, waiting for transfers between devices, per_device(): lax.all_to_all(out_part.reshape(doc_devices, own_rows, out_width), ('mp',...  11.1 us
    dot_general x1, matrix products, per_device(): lax.dot_general(col_block, all_docs, (((0,), (0,)), ((), ())), precision=...  4.83 us
    all_to_all x1, starting transfers between devices, per_device(): lax.all_to_all(out_part.reshape(doc_devices, own_rows, out_width), ('mp',...  4.18 us
    all_to_all x1, starting transfers between devices, per_device(): lax.all_to_all(jnp.broadcast_to(score_part[None], (layers,) + score_part....  4.06 us
    all_to_all x1, starting transfers between devices, per_device(): lax.all_to_all(jnp.broadcast_to(projected, (doc_devices, projected.shape[...  3.89 us
  transfers between devices with their start and end apart: 3, of which 3 were waited for; matrix products, arithmetic and copies ran while one was open for 3% of the time, Pallas kernels for 0%

profile of v8, /device:TPU:0, one launch (start us, length us, event | category | flops | bytes accessed | tf_op | source)
XLA Modules:
  0.0 190.6 jit_solution(11195739387255236685)
XLA Ops:
  0.6 0.0 copy-start
  0.6 1.3 slice_bitcast_fusion.3
  2.0 0.1 pad_maximum_fusion
  2.1 1.1 broadcast_in_dim.8
  3.2 0.0 copy-start.1
  3.2 107.9 %all_to_all.24 = bf16[128,16,2048]{2,1,0:T(8,128)(2,1)} all-to-all(bf16[128,16,2048]{2,1,0:T(8,128)(2,1)S(1)} %bitcast.41), channel_id=1, replica_groups=mesh['mp'=8,'layer'=4,'example'=4] {'mp','example','layer'}, dimensions={0} | all-to-all | bytes 16777216 | tf_op jit(solution)/shard_map/all_to_all | solution.py:87
  111.1 0.0 copy-done.1
  111.1 28.4 %shard_map.104 = f32[2048,64]{1,0:T(8,128)S(1)} custom-call(bf16[2048,2048]{1,0:T(8,128)(2,1)} %bitcast.42, bf16[1792,2048]{1,0:T(8,128)(2,1)} %bitcast.43, bf16[8,4,4,16,1792]{4,3,2,1,0:T(8,128)(2,1)} %bitcast.44, bf16[64,1792]{1,0:T(8,128)(2,1)S(1)} %bitcast.40), custom_call_target="tpu_custom_call" | custom-call | tf_op jit(solution)/shard_map/pallas_call | solution.py:51
  139.5 0.0 copy-start.2
  139.5 1.4 reshape.72
  140.9 4.2 %all-to-all-start.1 = ((f32[32,1,4096]{2,1,0:T(1,128)}), f32[32,1,4096]{2,1,0:T(1,128)S(1)}, u32[]{:S(2)}, u32[]{:S(2)}) async-start(f32[32,1,4096]{2,1,0:T(1,128)} %reshape.72), calls=%async_computation.1 | async-start | bytes 1048576 | tf_op jit(solution)/shard_map/all_to_all | solution.py:96
  145.8 0.0 copy-done
  145.8 0.0 copy-done.2
  145.8 0.4 fusion.2
  146.2 11.1 %all-to-all-done.1 = f32[32,1,4096]{2,1,0:T(1,128)S(1)} async-done(((f32[32,1,4096]{2,1,0:T(1,128)}), f32[32,1,4096]{2,1,0:T(1,128)S(1)}, u32[]{:S(2)}, u32[]{:S(2)}) %all-to-all-start.1) | async-done | bytes 524320 | tf_op jit(solution)/shard_map/all_to_all | solution.py:96
  157.4 0.6 broadcast.31
  157.9 1.9 %reduce = f32[32,4096]{1,0:T(8,128)S(1)} reduce(f32[32,1,4096]{2,1,0:T(1,128)S(1)} %all-to-all-done.1, f32[]{:T(128)} %broadcast.31), dimensions={1}, to_apply=%all_to_all.16.reduce_sub_computation | reduce | bytes 1048580 | tf_op jit(solution)/shard_map/all_to_all | solution.py:96
  159.9 0.0 copy-start.3
  159.9 0.4 reshape.73
  160.3 0.1 reduce_sum.18
  160.4 0.3 convolution_multiply_fusion.1
  160.7 0.1 mul.39
  160.8 1.3 broadcast_in_dim.9
  162.1 3.9 %all-to-all-start.2 = ((f32[32,1,4096]{2,1,0:T(1,128)}), f32[32,1,4096]{2,1,0:T(1,128)S(1)}, u32[]{:S(2)}, u32[]{:S(2)}) async-start(f32[32,1,4096]{2,1,0:T(1,128)} %broadcast_in_dim.9), calls=%async_computation.2 | async-start | bytes 1048576 | tf_op jit(solution)/shard_map/all_to_all | solution.py:121
  166.0 12.2 %all-to-all-done.2 = f32[32,1,4096]{2,1,0:T(1,128)S(1)} async-done(((f32[32,1,4096]{2,1,0:T(1,128)}), f32[32,1,4096]{2,1,0:T(1,128)S(1)}, u32[]{:S(2)}, u32[]{:S(2)}) %all-to-all-start.2) | async-done | bytes 524320 | tf_op jit(solution)/shard_map/all_to_all | solution.py:121
  178.2 0.0 copy-done.3
  178.2 0.7 convolution_bitcast_fusion
  178.9 0.1 copy.12
  179.0 0.7 reshape.74
  179.7 4.1 %all-to-all-start.3 = ((f32[4,1,1024]{2,1,0:T(1,128)}), f32[4,1,1024]{2,1,0:T(1,128)S(1)}, u32[]{:S(2)}, u32[]{:S(2)}) async-start(f32[4,1,1024]{2,1,0:T(1,128)} %reshape.74), calls=%async_computation.3 | async-start | bytes 32768 | tf_op jit(solution)/shard_map/all_to_all | solution.py:144
  183.8 4.8 %fusion.1 = f32[1,128,4096]{2,1,0:T(8,128)} fusion(f32[32,128]{1,0:T(8,128)S(1)} %bitcast.45, f32[1,128,4096]{2,1,0:T(8,128)} %param.16, f32[32,1,4096]{2,1,0:T(1,128)S(1)} %all-to-all-done.2), kind=kOutput, calls=%fused_computation.2 | convolution fusion | flops 202375168 | bytes 4734976 | tf_op jit(solution)/shard_map/dot_general | solution.py:132
  188.6 0.5 all-to-all-done.3
  189.1 0.7 reduce.1
  189.8 0.1 reshape.75
  189.9 0.6 reduce_sum.19
  (3 shorter events, 0.0 us)
Async XLA Ops:
  0.6 145.1 %copy-start = (bf16[1,64,8192]{2,1,0:T(8,128)(2,1)S(1)}, bf16[1,64,8192]{2,1,0:T(8,128)(2,1)}, u32[]{:S(2)}) copy-start(bf16[1,64,8192]{2,1,0:T(8,128)(2,1)} %param.14) | copy-start | bytes 3145732
  3.2 107.9 %copy-start.1 = (bf16[1,64,1792]{2,1,0:T(8,128)(2,1)S(1)}, bf16[1,64,1792]{2,1,0:T(8,128)(2,1)}, u32[]{:S(2)}) copy-start(bf16[1,64,1792]{2,1,0:T(8,128)(2,1)} %param.13) | copy-start | bytes 688132
  139.5 6.3 %copy-start.2 = (bf16[1,64,8192]{2,1,0:T(8,128)(2,1)S(1)}, bf16[1,64,8192]{2,1,0:T(8,128)(2,1)}, u32[]{:S(2)}) copy-start(bf16[1,64,8192]{2,1,0:T(8,128)(2,1)} %param.12) | copy-start | bytes 3145732
  140.9 16.4 %all-to-all-start.1 = ((f32[32,1,4096]{2,1,0:T(1,128)}), f32[32,1,4096]{2,1,0:T(1,128)S(1)}, u32[]{:S(2)}, u32[]{:S(2)}) async-start(f32[32,1,4096]{2,1,0:T(1,128)} %reshape.72), calls=%async_computation.1 | async-start | bytes 1048576 | tf_op jit(solution)/shard_map/all_to_all | solution.py:96
  159.9 18.3 %copy-start.3 = (bf16[1,32,4096]{2,1,0:T(8,128)(2,1)S(1)}, bf16[1,32,4096]{2,1,0:T(8,128)(2,1)}, u32[]{:S(2)}) copy-start(bf16[1,32,4096]{2,1,0:T(8,128)(2,1)} %param.15) | copy-start | bytes 786436
  162.1 16.2 %all-to-all-start.2 = ((f32[32,1,4096]{2,1,0:T(1,128)}), f32[32,1,4096]{2,1,0:T(1,128)S(1)}, u32[]{:S(2)}, u32[]{:S(2)}) async-start(f32[32,1,4096]{2,1,0:T(1,128)} %broadcast_in_dim.9), calls=%async_computation.2 | async-start | bytes 1048576 | tf_op jit(solution)/shard_map/all_to_all | solution.py:121
  179.7 9.4 %all-to-all-start.3 = ((f32[4,1,1024]{2,1,0:T(1,128)}), f32[4,1,1024]{2,1,0:T(1,128)S(1)}, u32[]{:S(2)}, u32[]{:S(2)}) async-start(f32[4,1,1024]{2,1,0:T(1,128)} %reshape.74), calls=%async_computation.3 | async-start | bytes 32768 | tf_op jit(solution)/shard_map/all_to_all | solution.py:144

commit v9 on v8

--- a/solution.py
+++ b/solution.py
@@ -94,13 +94,13 @@
     out_part = _up_project(token_cols, down_weight[0], gate5, proj_out[0])
     doc_devices = lax.axis_size(("mp", "example"))
     gathered = lax.all_to_all(
-        out_part.reshape(doc_devices, own_rows, out_width),
+        out_part.reshape(doc_devices, 8, own_rows * out_width // 8),
         ("mp", "example"),
         split_axis=0,
         concat_axis=0,
         tiled=True,
     )
-    out_rows = jnp.sum(gathered, axis=0)
+    out_rows = jnp.sum(gathered, axis=0).reshape(own_rows, out_width)
     in_rows = lax.dot_general(
         layer_input[0], proj_in[0], (((1,), (1,)), ((), ())), preferred_element_type=jnp.float32
     )

time: 191 us -> 188 us (0.984)
  other arithmetic: 3.52 us -> 1.49 us
    all_to_all x1 -> x0, other arithmetic: 1.94 us -> none  [per_device(): lax.all_to_all(out_part.reshape(doc_devices, own_rows, out_width), ('mp',...]
where the time goes in v9:
time: 188 us
  blocking collectives  108 us (57%)
  Pallas kernels  28.4 us (15%)
  waiting for transfers between devices  23.9 us (13%)
  starting transfers between devices  12.1 us (6%)
  local copies, waits for them, and re-layouts  6.31 us (3%)
  matrix products  6.21 us (3%)
    all_to_all x1, blocking collectives, per_device(): lax.all_to_all(pieces, ('mp', 'example', 'layer'), split_axis=0, concat_a...  108 us
    pallas_call x1, Pallas kernels, _up_project(): pl.pallas_call(_up_kernel, grid=(blocks,), in_specs=[pl.BlockSpec((tile,...  28.4 us
    all_to_all x1, waiting for transfers between devices, per_device(): lax.all_to_all(jnp.broadcast_to(projected, (doc_devices, projected.shape[...  12.2 us
    all_to_all x1, waiting for transfers between devices, per_device(): lax.all_to_all(out_part.reshape(doc_devices, 8, own_rows * out_width // 8...  11.1 us
    dot_general x1, matrix products, per_device(): lax.dot_general(col_block, all_docs, (((0,), (0,)), ((), ())), precision=...  4.83 us
    all_to_all x1, starting transfers between devices, per_device(): lax.all_to_all(out_part.reshape(doc_devices, 8, own_rows * out_width // 8...  4.18 us
    all_to_all x1, starting transfers between devices, per_device(): lax.all_to_all(jnp.broadcast_to(score_part[None], (layers,) + score_part....  4.06 us
    all_to_all x1, starting transfers between devices, per_device(): lax.all_to_all(jnp.broadcast_to(projected, (doc_devices, projected.shape[...  3.89 us
  transfers between devices with their start and end apart: 3, of which 3 were waited for; matrix products, arithmetic and copies ran while one was open for 3% of the time, Pallas kernels for 0%

profile of v9, /device:TPU:0, one launch (start us, length us, event | category | flops | bytes accessed | tf_op | source)
XLA Modules:
  0.0 187.7 jit_solution(4488329037879935600)
XLA Ops:
  0.6 0.0 copy-start
  0.6 1.3 slice_bitcast_fusion.3
  2.0 0.1 pad_maximum_fusion
  2.1 1.1 broadcast_in_dim.8
  3.2 0.0 copy-start.1
  3.2 107.9 %all_to_all.24 = bf16[128,16,2048]{2,1,0:T(8,128)(2,1)} all-to-all(bf16[128,16,2048]{2,1,0:T(8,128)(2,1)S(1)} %bitcast.39), channel_id=1, replica_groups=mesh['mp'=8,'layer'=4,'example'=4] {'mp','example','layer'}, dimensions={0} | all-to-all | bytes 16777216 | tf_op jit(solution)/shard_map/all_to_all | solution.py:87
  111.1 0.0 copy-done.1
  111.1 28.4 %shard_map.104 = f32[2048,64]{1,0:T(8,128)S(1)} custom-call(bf16[2048,2048]{1,0:T(8,128)(2,1)} %bitcast.40, bf16[1792,2048]{1,0:T(8,128)(2,1)} %bitcast.41, bf16[8,4,4,16,1792]{4,3,2,1,0:T(8,128)(2,1)} %bitcast.42, bf16[64,1792]{1,0:T(8,128)(2,1)S(1)} %bitcast.38), custom_call_target="tpu_custom_call" | custom-call | tf_op jit(solution)/shard_map/pallas_call | solution.py:51
  139.5 0.0 copy-start.2
  139.5 1.1 reshape.67
  140.5 4.2 %all-to-all-start.1 = ((f32[32,8,512]{2,1,0:T(8,128)}), f32[32,8,512]{2,1,0:T(8,128)S(1)}, u32[]{:S(2)}, u32[]{:S(2)}) async-start(f32[32,8,512]{2,1,0:T(8,128)} %reshape.67), calls=%async_computation.1 | async-start | bytes 1048576 | tf_op jit(solution)/shard_map/all_to_all | solution.py:96
  145.4 0.0 copy-done
  145.4 0.0 copy-done.2
  145.4 0.0 copy-start.3
  145.4 0.4 fusion.2
  145.8 11.1 %all-to-all-done.1 = f32[32,8,512]{2,1,0:T(8,128)S(1)} async-done(((f32[32,8,512]{2,1,0:T(8,128)}), f32[32,8,512]{2,1,0:T(8,128)S(1)}, u32[]{:S(2)}, u32[]{:S(2)}) %all-to-all-start.1) | async-done | bytes 524320 | tf_op jit(solution)/shard_map/all_to_all | solution.py:96
  157.0 0.1 reduce_sum.21
  157.1 0.3 convolution_multiply_fusion.1
  157.4 0.1 mul.37
  157.5 1.3 broadcast_in_dim.9
  158.8 3.9 %all-to-all-start.2 = ((f32[32,1,4096]{2,1,0:T(1,128)}), f32[32,1,4096]{2,1,0:T(1,128)S(1)}, u32[]{:S(2)}, u32[]{:S(2)}) async-start(f32[32,1,4096]{2,1,0:T(1,128)} %broadcast_in_dim.9), calls=%async_computation.2 | async-start | bytes 1048576 | tf_op jit(solution)/shard_map/all_to_all | solution.py:121
  162.7 12.2 %all-to-all-done.2 = f32[32,1,4096]{2,1,0:T(1,128)S(1)} async-done(((f32[32,1,4096]{2,1,0:T(1,128)}), f32[32,1,4096]{2,1,0:T(1,128)S(1)}, u32[]{:S(2)}, u32[]{:S(2)}) %all-to-all-start.2) | async-done | bytes 524320 | tf_op jit(solution)/shard_map/all_to_all | solution.py:121
  174.9 0.0 copy-done.3
  174.9 0.7 convolution_bitcast_fusion
  175.6 0.1 copy.13
  175.7 0.7 reshape.68
  176.4 4.1 %all-to-all-start.3 = ((f32[4,1,1024]{2,1,0:T(1,128)}), f32[4,1,1024]{2,1,0:T(1,128)S(1)}, u32[]{:S(2)}, u32[]{:S(2)}) async-start(f32[4,1,1024]{2,1,0:T(1,128)} %reshape.68), calls=%async_computation.3 | async-start | bytes 32768 | tf_op jit(solution)/shard_map/all_to_all | solution.py:144
  180.4 4.8 %fusion.1 = f32[1,128,4096]{2,1,0:T(8,128)} fusion(f32[32,128]{1,0:T(8,128)S(1)} %bitcast.43, f32[1,128,4096]{2,1,0:T(8,128)} %param.16, f32[32,1,4096]{2,1,0:T(1,128)S(1)} %all-to-all-done.2), kind=kOutput, calls=%fused_computation.2 | convolution fusion | flops 202375168 | bytes 4734976 | tf_op jit(solution)/shard_map/dot_general | solution.py:132
  185.3 0.5 all-to-all-done.3
  185.8 0.5 broadcast.28
  186.3 0.7 reduce
  187.0 0.1 reshape.69
  187.1 0.6 reduce_sum.22
  (4 shorter events, 0.1 us)
Async XLA Ops:
  0.6 144.8 %copy-start = (bf16[1,64,8192]{2,1,0:T(8,128)(2,1)S(1)}, bf16[1,64,8192]{2,1,0:T(8,128)(2,1)}, u32[]{:S(2)}) copy-start(bf16[1,64,8192]{2,1,0:T(8,128)(2,1)} %param.14) | copy-start | bytes 3145732
  3.2 107.9 %copy-start.1 = (bf16[1,64,1792]{2,1,0:T(8,128)(2,1)S(1)}, bf16[1,64,1792]{2,1,0:T(8,128)(2,1)}, u32[]{:S(2)}) copy-start(bf16[1,64,1792]{2,1,0:T(8,128)(2,1)} %param.13) | copy-start | bytes 688132
  139.5 5.9 %copy-start.2 = (bf16[1,64,8192]{2,1,0:T(8,128)(2,1)S(1)}, bf16[1,64,8192]{2,1,0:T(8,128)(2,1)}, u32[]{:S(2)}) copy-start(bf16[1,64,8192]{2,1,0:T(8,128)(2,1)} %param.12) | copy-start | bytes 3145732
  140.5 16.4 %all-to-all-start.1 = ((f32[32,8,512]{2,1,0:T(8,128)}), f32[32,8,512]{2,1,0:T(8,128)S(1)}, u32[]{:S(2)}, u32[]{:S(2)}) async-start(f32[32,8,512]{2,1,0:T(8,128)} %reshape.67), calls=%async_computation.1 | async-start | bytes 1048576 | tf_op jit(solution)/shard_map/all_to_all | solution.py:96
  145.4 29.5 %copy-start.3 = (bf16[1,32,4096]{2,1,0:T(8,128)(2,1)S(1)}, bf16[1,32,4096]{2,1,0:T(8,128)(2,1)}, u32[]{:S(2)}) copy-start(bf16[1,32,4096]{2,1,0:T(8,128)(2,1)} %param.15) | copy-start | bytes 786436
  158.8 16.2 %all-to-all-start.2 = ((f32[32,1,4096]{2,1,0:T(1,128)}), f32[32,1,4096]{2,1,0:T(1,128)S(1)}, u32[]{:S(2)}, u32[]{:S(2)}) async-start(f32[32,1,4096]{2,1,0:T(1,128)} %broadcast_in_dim.9), calls=%async_computation.2 | async-start | bytes 1048576 | tf_op jit(solution)/shard_map/all_to_all | solution.py:121
  176.4 9.4 %all-to-all-start.3 = ((f32[4,1,1024]{2,1,0:T(1,128)}), f32[4,1,1024]{2,1,0:T(1,128)S(1)}, u32[]{:S(2)}, u32[]{:S(2)}) async-start(f32[4,1,1024]{2,1,0:T(1,128)} %reshape.68), calls=%async_computation.3 | async-start | bytes 32768 | tf_op jit(solution)/shard_map/all_to_all | solution.py:144

commit v10 on v9

--- a/solution.py
+++ b/solution.py
@@ -118,13 +118,14 @@
         )
         * doc_scale
     )
+    doc_width = projected.shape[1]
     all_docs = lax.all_to_all(
-        jnp.broadcast_to(projected, (doc_devices, projected.shape[1])),
+        jnp.broadcast_to(projected.reshape(1, 8, doc_width // 8), (doc_devices, 8, doc_width // 8)),
         ("mp", "example"),
         split_axis=0,
         concat_axis=0,
         tiled=True,
-    )
+    ).reshape(doc_devices, doc_width)
     doc_total = all_docs.shape[0]
     block_rows = hessian_prior.shape[1]
     first_col = lax.axis_index(("mp", "example")) * block_rows
@@ -140,16 +141,17 @@
         precision=lax.Precision.HIGHEST,
     )
     layers = lax.axis_size("layer")
+    score_size = score_part.size
     scores = jnp.sum(
         lax.all_to_all(
-            jnp.broadcast_to(score_part[None], (layers,) + score_part.shape),
+            jnp.broadcast_to(score_part.reshape(1, 8, score_size // 8), (layers, 8, score_size // 8)),
             "layer",
             split_axis=0,
             concat_axis=0,
             tiled=True,
         ),
         axis=0,
-    )
+    ).reshape(score_part.shape)
     return (hessian[None], scores)
 
 

time: 188 us -> 187 us (level)
  no operation moved by 1% of the time
where the time goes in v10:
time: 187 us; the launch traced here: 186 us
  blocking collectives  108 us (58%)
  Pallas kernels  28.4 us (15%)
  waiting for transfers between devices  24 us (13%)
  starting transfers between devices  12.1 us (6%)
  local copies, waits for them, and re-layouts  6.24 us (3%)
  matrix products  5.88 us (3%)
    all_to_all x1, blocking collectives, per_device(): lax.all_to_all(pieces, ('mp', 'example', 'layer'), split_axis=0, concat_a...  108 us
    pallas_call x1, Pallas kernels, _up_project(): pl.pallas_call(_up_kernel, grid=(blocks,), in_specs=[pl.BlockSpec((tile,...  28.4 us
    all_to_all x1, waiting for transfers between devices, per_device(): lax.all_to_all(jnp.broadcast_to(projected.reshape(1, 8, doc_width // 8),...  12.2 us
    all_to_all x1, waiting for transfers between devices, per_device(): lax.all_to_all(out_part.reshape(doc_devices, 8, own_rows * out_width // 8...  11.1 us
    dot_general x1, matrix products, per_device(): lax.dot_general(col_block, all_docs, (((0,), (0,)), ((), ())), precision=...  4.79 us
    all_to_all x1, starting transfers between devices, per_device(): lax.all_to_all(out_part.reshape(doc_devices, 8, own_rows * out_width // 8...  4.18 us
    all_to_all x1, starting transfers between devices, per_device(): lax.all_to_all(jnp.broadcast_to(score_part.reshape(1, 8, score_size // 8)...  4.06 us
    all_to_all x1, starting transfers between devices, per_device(): lax.all_to_all(jnp.broadcast_to(projected.reshape(1, 8, doc_width // 8),...  3.89 us
  transfers between devices with their start and end apart: 3, of which 3 were waited for; matrix products, arithmetic and copies ran while one was open for 3% of the time, Pallas kernels for 0%

profile of v10, /device:TPU:0, one launch (start us, length us, event | category | flops | bytes accessed | tf_op | source)
XLA Modules:
  0.0 186.1 jit_solution(13772867257521227427)
XLA Ops:
  0.6 0.0 copy-start
  0.6 1.3 slice_bitcast_fusion.3
  2.0 0.1 pad_maximum_fusion
  2.1 1.1 broadcast_in_dim.10
  3.2 0.0 copy-start.1
  3.2 107.9 %all_to_all.20 = bf16[128,16,2048]{2,1,0:T(8,128)(2,1)} all-to-all(bf16[128,16,2048]{2,1,0:T(8,128)(2,1)S(1)} %bitcast.36), channel_id=1, replica_groups=mesh['mp'=8,'layer'=4,'example'=4] {'mp','example','layer'}, dimensions={0} | all-to-all | bytes 16777216 | tf_op jit(solution)/shard_map/all_to_all | solution.py:87
  111.1 0.0 copy-done.1
  111.1 28.4 %shard_map.104 = f32[2048,64]{1,0:T(8,128)S(1)} custom-call(bf16[2048,2048]{1,0:T(8,128)(2,1)} %bitcast.37, bf16[1792,2048]{1,0:T(8,128)(2,1)} %bitcast.38, bf16[8,4,4,16,1792]{4,3,2,1,0:T(8,128)(2,1)} %bitcast.39, bf16[64,1792]{1,0:T(8,128)(2,1)S(1)} %bitcast.35), custom_call_target="tpu_custom_call" | custom-call | tf_op jit(solution)/shard_map/pallas_call | solution.py:51
  139.5 0.0 copy-start.2
  139.5 1.1 reshape.69
  140.5 4.2 %all-to-all-start.1 = ((f32[32,8,512]{2,1,0:T(8,128)}), f32[32,8,512]{2,1,0:T(8,128)S(1)}, u32[]{:S(2)}, u32[]{:S(2)}) async-start(f32[32,8,512]{2,1,0:T(8,128)} %reshape.69), calls=%async_computation.1 | async-start | bytes 1048576 | tf_op jit(solution)/shard_map/all_to_all | solution.py:96
  145.4 0.0 copy-done
  145.4 0.0 copy-done.2
  145.4 0.4 fusion.2
  145.8 0.0 copy-start.3
  145.8 11.1 %all-to-all-done.1 = f32[32,8,512]{2,1,0:T(8,128)S(1)} async-done(((f32[32,8,512]{2,1,0:T(8,128)}), f32[32,8,512]{2,1,0:T(8,128)S(1)}, u32[]{:S(2)}, u32[]{:S(2)}) %all-to-all-start.1) | async-done | bytes 524320 | tf_op jit(solution)/shard_map/all_to_all | solution.py:96
  157.0 0.1 reduce_sum.21
  157.1 0.3 convolution_multiply_fusion.1
  157.4 0.1 mul.38
  157.5 0.9 broadcast_in_dim.11
  158.3 3.9 %all-to-all-start.2 = ((f32[32,8,512]{2,1,0:T(8,128)}), f32[32,8,512]{2,1,0:T(8,128)S(1)}, u32[]{:S(2)}, u32[]{:S(2)}) async-start(f32[32,8,512]{2,1,0:T(8,128)} %broadcast_in_dim.11), calls=%async_computation.2 | async-start | bytes 1048576 | tf_op jit(solution)/shard_map/all_to_all | solution.py:122
  162.2 12.2 %all-to-all-done.2 = f32[32,8,512]{2,1,0:T(8,128)S(1)} async-done(((f32[32,8,512]{2,1,0:T(8,128)}), f32[32,8,512]{2,1,0:T(8,128)S(1)}, u32[]{:S(2)}, u32[]{:S(2)}) %all-to-all-start.2) | async-done | bytes 524320 | tf_op jit(solution)/shard_map/all_to_all | solution.py:122
  174.5 0.3 copy.13
  174.8 0.0 copy-done.3
  174.8 0.4 convolution_bitcast_fusion
  175.2 0.1 copy.12
  175.3 0.1 broadcast_in_dim.13
  175.3 0.6 broadcast_in_dim.28
  176.0 4.1 %all-to-all-start.3 = ((f32[4,8,128]{2,1,0:T(8,128)}), f32[4,8,128]{2,1,0:T(8,128)S(1)}, u32[]{:S(2)}, u32[]{:S(2)}) async-start(f32[4,8,128]{2,1,0:T(8,128)} %broadcast_in_dim.28), calls=%async_computation.3 | async-start | bytes 32768 | tf_op jit(solution)/shard_map/all_to_all | solution.py:146
  180.0 4.8 %fusion.1 = f32[1,128,4096]{2,1,0:T(8,128)} fusion(f32[32,4096]{1,0:T(8,128)S(1)} %bitcast.41, f32[1,128,4096]{2,1,0:T(8,128)} %param.16, s32[]{:T(128)S(6)} %select_n.3), kind=kOutput, calls=%fused_computation.2 | convolution fusion | flops 202375168 | bytes 4734980 | tf_op jit(solution)/shard_map/dot_general | solution.py:133
  184.8 0.6 all-to-all-done.3
  185.4 0.7 reshape.71
  (3 shorter events, 0.1 us)
Async XLA Ops:
  0.6 144.8 %copy-start = (bf16[1,64,8192]{2,1,0:T(8,128)(2,1)S(1)}, bf16[1,64,8192]{2,1,0:T(8,128)(2,1)}, u32[]{:S(2)}) copy-start(bf16[1,64,8192]{2,1,0:T(8,128)(2,1)} %param.14) | copy-start | bytes 3145732
  3.2 107.9 %copy-start.1 = (bf16[1,64,1792]{2,1,0:T(8,128)(2,1)S(1)}, bf16[1,64,1792]{2,1,0:T(8,128)(2,1)}, u32[]{:S(2)}) copy-start(bf16[1,64,1792]{2,1,0:T(8,128)(2,1)} %param.13) | copy-start | bytes 688132
  139.5 5.9 %copy-start.2 = (bf16[1,64,8192]{2,1,0:T(8,128)(2,1)S(1)}, bf16[1,64,8192]{2,1,0:T(8,128)(2,1)}, u32[]{:S(2)}) copy-start(bf16[1,64,8192]{2,1,0:T(8,128)(2,1)} %param.12) | copy-start | bytes 3145732
  140.5 16.4 %all-to-all-start.1 = ((f32[32,8,512]{2,1,0:T(8,128)}), f32[32,8,512]{2,1,0:T(8,128)S(1)}, u32[]{:S(2)}, u32[]{:S(2)}) async-start(f32[32,8,512]{2,1,0:T(8,128)} %reshape.69), calls=%async_computation.1 | async-start | bytes 1048576 | tf_op jit(solution)/shard_map/all_to_all | solution.py:96
  145.8 29.0 %copy-start.3 = (bf16[1,32,4096]{2,1,0:T(8,128)(2,1)S(1)}, bf16[1,32,4096]{2,1,0:T(8,128)(2,1)}, u32[]{:S(2)}) copy-start(bf16[1,32,4096]{2,1,0:T(8,128)(2,1)} %param.15) | copy-start | bytes 786436
  158.3 16.2 %all-to-all-start.2 = ((f32[32,8,512]{2,1,0:T(8,128)}), f32[32,8,512]{2,1,0:T(8,128)S(1)}, u32[]{:S(2)}, u32[]{:S(2)}) async-start(f32[32,8,512]{2,1,0:T(8,128)} %broadcast_in_dim.11), calls=%async_computation.2 | async-start | bytes 1048576 | tf_op jit(solution)/shard_map/all_to_all | solution.py:122
  176.0 9.4 %all-to-all-start.3 = ((f32[4,8,128]{2,1,0:T(8,128)}), f32[4,8,128]{2,1,0:T(8,128)S(1)}, u32[]{:S(2)}, u32[]{:S(2)}) async-start(f32[4,8,128]{2,1,0:T(8,128)} %broadcast_in_dim.28), calls=%async_computation.3 | async-start | bytes 32768 | tf_op jit(solution)/shard_map/all_to_all | solution.py:146

commit v11 on v10

--- a/solution.py
+++ b/solution.py
@@ -6,7 +6,7 @@
 from jax.experimental.pallas import tpu as pltpu
 
 
-def _up_kernel(cot_ref, w_ref, gate_ref, proj_ref, out_ref):
+def _up_kernel(cot_ref, w_ref, gate_ref, proj_ref, out_ref, order_ref):
     hidden = lax.dot_general(
         cot_ref[...], w_ref[...], (((1,), (1,)), ((), ())), preferred_element_type=jnp.float32
     )
@@ -29,7 +29,7 @@
         high, proj, dims, preferred_element_type=jnp.float32
     ) + lax.dot_general(low, proj, dims, preferred_element_type=jnp.float32)
     rows = gate_ref.shape[3]
-    out_ref[...] = jnp.concatenate(
+    order_ref[...] = jnp.concatenate(
         [
             result[((b * groups + e) * layers + l) * rows :][:rows]
             for b in range(blocks)
@@ -38,9 +38,15 @@
         ],
         axis=0,
     )
+    docs, bands, _ = out_ref.shape
+    step = order_ref.shape[0] // (docs * bands)
+    width = order_ref.shape[1]
+    for q in range(step):
+        part = order_ref[pl.ds(q, docs * bands, stride=step), :]
+        out_ref[:, :, q * width : (q + 1) * width] = part.reshape(docs, bands, width)
 
 
-def _up_project(token_cols, weight, gate5, proj):
+def _up_project(token_cols, weight, gate5, proj, seq):
     tokens, feats = token_cols.shape
     hidden = weight.shape[0]
     width = proj.shape[0]
@@ -57,8 +63,9 @@
             pl.BlockSpec((per_tile, layers, groups, rows, hidden), lambda i: (i, 0, 0, 0, 0)),
             pl.BlockSpec((width, hidden), lambda i: (0, 0)),
         ],
-        out_specs=pl.BlockSpec((tile, width), lambda i: (i, 0)),
-        out_shape=jax.ShapeDtypeStruct((tokens, width), jnp.float32),
+        out_specs=pl.BlockSpec((tile // seq, 8, seq * width // 8), lambda i: (i, 0, 0)),
+        out_shape=jax.ShapeDtypeStruct((tokens // seq, 8, seq * width // 8), jnp.float32),
+        scratch_shapes=[pltpu.VMEM((tile, width), jnp.float32)],
         compiler_params=pltpu.CompilerParams(vmem_limit_bytes=48 * 1024 * 1024),
     )(token_cols, weight, gate5, proj)
 
@@ -91,7 +98,7 @@
     out_width = proj_out.shape[1]
     own_rows = layer_input.shape[1]
     gate5 = gate_act[0].reshape(shares, layer_count, groups, local_rows, gate_act.shape[2])
-    out_part = _up_project(token_cols, down_weight[0], gate5, proj_out[0])
+    out_part = _up_project(token_cols, down_weight[0], gate5, proj_out[0], own_rows)
     doc_devices = lax.axis_size(("mp", "example"))
     gathered = lax.all_to_all(
         out_part.reshape(doc_devices, 8, own_rows * out_width // 8),

time: 187 us -> 187 us (level)
  no operation moved by 1% of the time
where the time goes in v11:
time: 187 us; the launch traced here: 186 us
  blocking collectives  108 us (58%)
  Pallas kernels  29.5 us (16%)
  waiting for transfers between devices  24 us (13%)
  starting transfers between devices  12.1 us (6%)
  matrix products  5.88 us (3%)
  local copies, waits for them, and re-layouts  5.18 us (3%)
    all_to_all x1, blocking collectives, per_device(): lax.all_to_all(pieces, ('mp', 'example', 'layer'), split_axis=0, concat_a...  108 us
    pallas_call x1, Pallas kernels, _up_project(): pl.pallas_call(_up_kernel, grid=(blocks,), in_specs=[pl.BlockSpec((tile,...  29.5 us
    all_to_all x1, waiting for transfers between devices, per_device(): lax.all_to_all(jnp.broadcast_to(projected.reshape(1, 8, doc_width // 8),...  12.2 us
    all_to_all x1, waiting for transfers between devices, per_device(): lax.all_to_all(out_part.reshape(doc_devices, 8, own_rows * out_width // 8...  11.1 us
    dot_general x1, matrix products, per_device(): lax.dot_general(col_block, all_docs, (((0,), (0,)), ((), ())), precision=...  4.79 us
    all_to_all x1, starting transfers between devices, per_device(): lax.all_to_all(out_part.reshape(doc_devices, 8, own_rows * out_width // 8...  4.18 us
    all_to_all x1, starting transfers between devices, per_device(): lax.all_to_all(jnp.broadcast_to(score_part.reshape(1, 8, score_size // 8)...  4.06 us
    all_to_all x1, starting transfers between devices, per_device(): lax.all_to_all(jnp.broadcast_to(projected.reshape(1, 8, doc_width // 8),...  3.89 us
  transfers between devices with their start and end apart: 3, of which 3 were waited for; matrix products, arithmetic and copies ran while one was open for 3% of the time, Pallas kernels for 0%

profile of v11, /device:TPU:0, one launch (start us, length us, event | category | flops | bytes accessed | tf_op | source)
XLA Modules:
  0.0 186.1 jit_solution(4516452238102534061)
XLA Ops:
  0.6 0.0 copy-start
  0.6 1.3 slice_bitcast_fusion.3
  2.0 0.1 pad_maximum_fusion
  2.1 1.1 broadcast_in_dim.10
  3.2 0.0 copy-start.1
  3.2 107.9 %all_to_all.20 = bf16[128,16,2048]{2,1,0:T(8,128)(2,1)} all-to-all(bf16[128,16,2048]{2,1,0:T(8,128)(2,1)S(1)} %bitcast.36), channel_id=1, replica_groups=mesh['mp'=8,'layer'=4,'example'=4] {'mp','example','layer'}, dimensions={0} | all-to-all | bytes 16777216 | tf_op jit(solution)/shard_map/all_to_all | solution.py:94
  111.1 0.0 copy-done.1
  111.1 0.0 copy-start.2
  111.1 29.5 %shard_map.104 = f32[32,8,512]{2,1,0:T(8,128)} custom-call(bf16[2048,2048]{1,0:T(8,128)(2,1)} %bitcast.37, bf16[1792,2048]{1,0:T(8,128)(2,1)} %bitcast.38, bf16[8,4,4,16,1792]{4,3,2,1,0:T(8,128)(2,1)} %bitcast.39, bf16[64,1792]{1,0:T(8,128)(2,1)S(1)} %bitcast.35), custom_call_target="tpu_custom_call" | custom-call | tf_op jit(solution)/shard_map/pallas_call | solution.py:57
  140.5 4.2 %all-to-all-start.1 = ((f32[32,8,512]{2,1,0:T(8,128)}), f32[32,8,512]{2,1,0:T(8,128)S(1)}, u32[]{:S(2)}, u32[]{:S(2)}) async-start(f32[32,8,512]{2,1,0:T(8,128)} %shard_map.104), calls=%async_computation.1 | async-start | bytes 1048576 | tf_op jit(solution)/shard_map/all_to_all | solution.py:103
  145.4 0.0 copy-done
  145.4 0.0 copy-done.2
  145.4 0.4 fusion.2
  145.8 0.0 copy-start.3
  145.8 11.1 %all-to-all-done.1 = f32[32,8,512]{2,1,0:T(8,128)S(1)} async-done(((f32[32,8,512]{2,1,0:T(8,128)}), f32[32,8,512]{2,1,0:T(8,128)S(1)}, u32[]{:S(2)}, u32[]{:S(2)}) %all-to-all-start.1) | async-done | bytes 524320 | tf_op jit(solution)/shard_map/all_to_all | solution.py:103
  157.0 0.1 reduce_sum.21
  157.1 0.3 convolution_multiply_fusion.1
  157.4 0.1 mul.38
  157.5 0.9 broadcast_in_dim.11
  158.3 3.9 %all-to-all-start.2 = ((f32[32,8,512]{2,1,0:T(8,128)}), f32[32,8,512]{2,1,0:T(8,128)S(1)}, u32[]{:S(2)}, u32[]{:S(2)}) async-start(f32[32,8,512]{2,1,0:T(8,128)} %broadcast_in_dim.11), calls=%async_computation.2 | async-start | bytes 1048576 | tf_op jit(solution)/shard_map/all_to_all | solution.py:129
  162.3 12.2 %all-to-all-done.2 = f32[32,8,512]{2,1,0:T(8,128)S(1)} async-done(((f32[32,8,512]{2,1,0:T(8,128)}), f32[32,8,512]{2,1,0:T(8,128)S(1)}, u32[]{:S(2)}, u32[]{:S(2)}) %all-to-all-start.2) | async-done | bytes 524320 | tf_op jit(solution)/shard_map/all_to_all | solution.py:129
  174.5 0.3 copy.13
  174.8 0.0 copy-done.3
  174.8 0.4 convolution_bitcast_fusion
  175.2 0.1 copy.12
  175.3 0.1 broadcast_in_dim.13
  175.3 0.6 broadcast_in_dim.28
  176.0 4.1 %all-to-all-start.3 = ((f32[4,8,128]{2,1,0:T(8,128)}), f32[4,8,128]{2,1,0:T(8,128)S(1)}, u32[]{:S(2)}, u32[]{:S(2)}) async-start(f32[4,8,128]{2,1,0:T(8,128)} %broadcast_in_dim.28), calls=%async_computation.3 | async-start | bytes 32768 | tf_op jit(solution)/shard_map/all_to_all | solution.py:153
  180.0 4.8 %fusion.1 = f32[1,128,4096]{2,1,0:T(8,128)} fusion(f32[32,4096]{1,0:T(8,128)S(1)} %bitcast.41, f32[1,128,4096]{2,1,0:T(8,128)} %param.16, s32[]{:T(128)S(6)} %select_n.3), kind=kOutput, calls=%fused_computation.2 | convolution fusion | flops 202375168 | bytes 4734980 | tf_op jit(solution)/shard_map/dot_general | solution.py:140
  184.8 0.6 all-to-all-done.3
  185.4 0.7 reshape.67
  (3 shorter events, 0.1 us)
Async XLA Ops:
  0.6 144.8 %copy-start = (bf16[1,64,8192]{2,1,0:T(8,128)(2,1)S(1)}, bf16[1,64,8192]{2,1,0:T(8,128)(2,1)}, u32[]{:S(2)}) copy-start(bf16[1,64,8192]{2,1,0:T(8,128)(2,1)} %param.14) | copy-start | bytes 3145732
  3.2 107.9 %copy-start.1 = (bf16[1,64,1792]{2,1,0:T(8,128)(2,1)S(1)}, bf16[1,64,1792]{2,1,0:T(8,128)(2,1)}, u32[]{:S(2)}) copy-start(bf16[1,64,1792]{2,1,0:T(8,128)(2,1)} %param.13) | copy-start | bytes 688132
  111.1 34.3 %copy-start.2 = (bf16[1,64,8192]{2,1,0:T(8,128)(2,1)S(1)}, bf16[1,64,8192]{2,1,0:T(8,128)(2,1)}, u32[]{:S(2)}) copy-start(bf16[1,64,8192]{2,1,0:T(8,128)(2,1)} %param.12) | copy-start | bytes 3145732
  140.5 16.4 %all-to-all-start.1 = ((f32[32,8,512]{2,1,0:T(8,128)}), f32[32,8,512]{2,1,0:T(8,128)S(1)}, u32[]{:S(2)}, u32[]{:S(2)}) async-start(f32[32,8,512]{2,1,0:T(8,128)} %shard_map.104), calls=%async_computation.1 | async-start | bytes 1048576 | tf_op jit(solution)/shard_map/all_to_all | solution.py:103
  145.8 29.0 %copy-start.3 = (bf16[1,32,4096]{2,1,0:T(8,128)(2,1)S(1)}, bf16[1,32,4096]{2,1,0:T(8,128)(2,1)}, u32[]{:S(2)}) copy-start(bf16[1,32,4096]{2,1,0:T(8,128)(2,1)} %param.15) | copy-start | bytes 786436
  158.3 16.2 %all-to-all-start.2 = ((f32[32,8,512]{2,1,0:T(8,128)}), f32[32,8,512]{2,1,0:T(8,128)S(1)}, u32[]{:S(2)}, u32[]{:S(2)}) async-start(f32[32,8,512]{2,1,0:T(8,128)} %broadcast_in_dim.11), calls=%async_computation.2 | async-start | bytes 1048576 | tf_op jit(solution)/shard_map/all_to_all | solution.py:129
  176.0 9.4 %all-to-all-start.3 = ((f32[4,8,128]{2,1,0:T(8,128)}), f32[4,8,128]{2,1,0:T(8,128)S(1)}, u32[]{:S(2)}, u32[]{:S(2)}) async-start(f32[4,8,128]{2,1,0:T(8,128)} %broadcast_in_dim.28), calls=%async_computation.3 | async-start | bytes 32768 | tf_op jit(solution)/shard_map/all_to_all | solution.py:153

commit v12 on v11

--- a/solution.py
+++ b/solution.py
@@ -51,7 +51,7 @@
     hidden = weight.shape[0]
     width = proj.shape[0]
     shares, layers, groups, rows = gate5.shape[:4]
-    per_tile = 2
+    per_tile = 4
     blocks = shares // per_tile
     tile = tokens // blocks
     return pl.pallas_call(

time: 187 us -> 188 us (level)
  no operation moved by 1% of the time
where the time goes in v12:
time: 188 us
  blocking collectives  108 us (57%)
  Pallas kernels  31 us (16%)
  waiting for transfers between devices  24 us (13%)
  starting transfers between devices  12.1 us (6%)
  matrix products  5.87 us (3%)
  local copies, waits for them, and re-layouts  5.18 us (3%)
    all_to_all x1, blocking collectives, per_device(): lax.all_to_all(pieces, ('mp', 'example', 'layer'), split_axis=0, concat_a...  108 us
    pallas_call x1, Pallas kernels, _up_project(): pl.pallas_call(_up_kernel, grid=(blocks,), in_specs=[pl.BlockSpec((tile,...  31 us
    all_to_all x1, waiting for transfers between devices, per_device(): lax.all_to_all(jnp.broadcast_to(projected.reshape(1, 8, doc_width // 8),...  12.2 us
    all_to_all x1, waiting for transfers between devices, per_device(): lax.all_to_all(out_part.reshape(doc_devices, 8, own_rows * out_width // 8...  11.1 us
    dot_general x1, matrix products, per_device(): lax.dot_general(col_block, all_docs, (((0,), (0,)), ((), ())), precision=...  4.79 us
    all_to_all x1, starting transfers between devices, per_device(): lax.all_to_all(out_part.reshape(doc_devices, 8, own_rows * out_width // 8...  4.18 us
    all_to_all x1, starting transfers between devices, per_device(): lax.all_to_all(jnp.broadcast_to(score_part.reshape(1, 8, score_size // 8)...  4.05 us
    all_to_all x1, starting transfers between devices, per_device(): lax.all_to_all(jnp.broadcast_to(projected.reshape(1, 8, doc_width // 8),...  3.89 us
  transfers between devices with their start and end apart: 3, of which 3 were waited for; matrix products, arithmetic and copies ran while one was open for 3% of the time, Pallas kernels for 0%

profile of v12, /device:TPU:0, one launch (start us, length us, event | category | flops | bytes accessed | tf_op | source)
XLA Modules:
  0.0 187.6 jit_solution(6195056544363404985)
XLA Ops:
  0.6 0.0 copy-start
  0.6 1.3 slice_bitcast_fusion.3
  2.0 0.1 pad_maximum_fusion
  2.1 1.1 broadcast_in_dim.10
  3.2 0.0 copy-start.1
  3.2 107.9 %all_to_all.20 = bf16[128,16,2048]{2,1,0:T(8,128)(2,1)} all-to-all(bf16[128,16,2048]{2,1,0:T(8,128)(2,1)S(1)} %bitcast.36), channel_id=1, replica_groups=mesh['mp'=8,'layer'=4,'example'=4] {'mp','example','layer'}, dimensions={0} | all-to-all | bytes 16777216 | tf_op jit(solution)/shard_map/all_to_all | solution.py:94
  111.1 0.0 copy-done.1
  111.1 0.0 copy-start.2
  111.1 31.0 %shard_map.104 = f32[32,8,512]{2,1,0:T(8,128)} custom-call(bf16[2048,2048]{1,0:T(8,128)(2,1)} %bitcast.37, bf16[1792,2048]{1,0:T(8,128)(2,1)} %bitcast.38, bf16[8,4,4,16,1792]{4,3,2,1,0:T(8,128)(2,1)} %bitcast.39, bf16[64,1792]{1,0:T(8,128)(2,1)S(1)} %bitcast.35), custom_call_target="tpu_custom_call" | custom-call | tf_op jit(solution)/shard_map/pallas_call | solution.py:57
  142.0 4.2 %all-to-all-start.1 = ((f32[32,8,512]{2,1,0:T(8,128)}), f32[32,8,512]{2,1,0:T(8,128)S(1)}, u32[]{:S(2)}, u32[]{:S(2)}) async-start(f32[32,8,512]{2,1,0:T(8,128)} %shard_map.104), calls=%async_computation.1 | async-start | bytes 1048576 | tf_op jit(solution)/shard_map/all_to_all | solution.py:103
  146.9 0.0 copy-done
  146.9 0.0 copy-done.2
  146.9 0.4 fusion.2
  147.3 0.0 copy-start.3
  147.3 11.1 %all-to-all-done.1 = f32[32,8,512]{2,1,0:T(8,128)S(1)} async-done(((f32[32,8,512]{2,1,0:T(8,128)}), f32[32,8,512]{2,1,0:T(8,128)S(1)}, u32[]{:S(2)}, u32[]{:S(2)}) %all-to-all-start.1) | async-done | bytes 524320 | tf_op jit(solution)/shard_map/all_to_all | solution.py:103
  158.5 0.1 reduce_sum.21
  158.6 0.3 convolution_multiply_fusion.1
  158.9 0.1 mul.38
  159.0 0.9 broadcast_in_dim.11
  159.8 3.9 %all-to-all-start.2 = ((f32[32,8,512]{2,1,0:T(8,128)}), f32[32,8,512]{2,1,0:T(8,128)S(1)}, u32[]{:S(2)}, u32[]{:S(2)}) async-start(f32[32,8,512]{2,1,0:T(8,128)} %broadcast_in_dim.11), calls=%async_computation.2 | async-start | bytes 1048576 | tf_op jit(solution)/shard_map/all_to_all | solution.py:129
  163.8 12.2 %all-to-all-done.2 = f32[32,8,512]{2,1,0:T(8,128)S(1)} async-done(((f32[32,8,512]{2,1,0:T(8,128)}), f32[32,8,512]{2,1,0:T(8,128)S(1)}, u32[]{:S(2)}, u32[]{:S(2)}) %all-to-all-start.2) | async-done | bytes 524320 | tf_op jit(solution)/shard_map/all_to_all | solution.py:129
  176.0 0.3 copy.13
  176.3 0.0 copy-done.3
  176.3 0.4 convolution_bitcast_fusion
  176.7 0.1 copy.12
  176.8 0.1 broadcast_in_dim.13
  176.8 0.6 broadcast_in_dim.28
  177.5 4.1 %all-to-all-start.3 = ((f32[4,8,128]{2,1,0:T(8,128)}), f32[4,8,128]{2,1,0:T(8,128)S(1)}, u32[]{:S(2)}, u32[]{:S(2)}) async-start(f32[4,8,128]{2,1,0:T(8,128)} %broadcast_in_dim.28), calls=%async_computation.3 | async-start | bytes 32768 | tf_op jit(solution)/shard_map/all_to_all | solution.py:153
  181.5 4.8 %fusion.1 = f32[1,128,4096]{2,1,0:T(8,128)} fusion(f32[32,4096]{1,0:T(8,128)S(1)} %bitcast.41, f32[1,128,4096]{2,1,0:T(8,128)} %param.16, s32[]{:T(128)S(6)} %select_n.3), kind=kOutput, calls=%fused_computation.2 | convolution fusion | flops 202375168 | bytes 4734980 | tf_op jit(solution)/shard_map/dot_general | solution.py:140
  186.3 0.6 all-to-all-done.3
  186.9 0.7 reshape.67
  (3 shorter events, 0.1 us)
Async XLA Ops:
  0.6 146.3 %copy-start = (bf16[1,64,8192]{2,1,0:T(8,128)(2,1)S(1)}, bf16[1,64,8192]{2,1,0:T(8,128)(2,1)}, u32[]{:S(2)}) copy-start(bf16[1,64,8192]{2,1,0:T(8,128)(2,1)} %param.14) | copy-start | bytes 3145732
  3.2 107.9 %copy-start.1 = (bf16[1,64,1792]{2,1,0:T(8,128)(2,1)S(1)}, bf16[1,64,1792]{2,1,0:T(8,128)(2,1)}, u32[]{:S(2)}) copy-start(bf16[1,64,1792]{2,1,0:T(8,128)(2,1)} %param.13) | copy-start | bytes 688132
  111.1 35.8 %copy-start.2 = (bf16[1,64,8192]{2,1,0:T(8,128)(2,1)S(1)}, bf16[1,64,8192]{2,1,0:T(8,128)(2,1)}, u32[]{:S(2)}) copy-start(bf16[1,64,8192]{2,1,0:T(8,128)(2,1)} %param.12) | copy-start | bytes 3145732
  142.0 16.4 %all-to-all-start.1 = ((f32[32,8,512]{2,1,0:T(8,128)}), f32[32,8,512]{2,1,0:T(8,128)S(1)}, u32[]{:S(2)}, u32[]{:S(2)}) async-start(f32[32,8,512]{2,1,0:T(8,128)} %shard_map.104), calls=%async_computation.1 | async-start | bytes 1048576 | tf_op jit(solution)/shard_map/all_to_all | solution.py:103
  147.3 29.0 %copy-start.3 = (bf16[1,32,4096]{2,1,0:T(8,128)(2,1)S(1)}, bf16[1,32,4096]{2,1,0:T(8,128)(2,1)}, u32[]{:S(2)}) copy-start(bf16[1,32,4096]{2,1,0:T(8,128)(2,1)} %param.15) | copy-start | bytes 786436
  159.8 16.2 %all-to-all-start.2 = ((f32[32,8,512]{2,1,0:T(8,128)}), f32[32,8,512]{2,1,0:T(8,128)S(1)}, u32[]{:S(2)}, u32[]{:S(2)}) async-start(f32[32,8,512]{2,1,0:T(8,128)} %broadcast_in_dim.11), calls=%async_computation.2 | async-start | bytes 1048576 | tf_op jit(solution)/shard_map/all_to_all | solution.py:129
  177.5 9.4 %all-to-all-start.3 = ((f32[4,8,128]{2,1,0:T(8,128)}), f32[4,8,128]{2,1,0:T(8,128)S(1)}, u32[]{:S(2)}, u32[]{:S(2)}) async-start(f32[4,8,128]{2,1,0:T(8,128)} %broadcast_in_dim.28), calls=%async_computation.3 | async-start | bytes 32768 | tf_op jit(solution)/shard_map/all_to_all | solution.py:153
